TPU v7x, 128 devices: a whole 4x4x4 slice. The times are simulated.
128 devices in a mesh: dom: 16 (over x, z), outer: 8 (over y, core).
Axes of the slice: x: 4, y: 4, z: 4, core: 2. Of those that a mesh axis runs over, the one named last changes fastest.
Arguments:
- jacobian: bfloat16 [16384, 7, 4096], P(('dom', 'outer')), may hold values from -0.25 to 0.25
- pod_basis: bfloat16 [16384, 4096], P(('dom', 'outer')), may hold values from -6 to 6
- ghost_rows: int32 [128, 128, 4], P(None, ('dom', 'outer')), may hold values from 0 to 127, as said below
- column_slot: int32 [16384, 7], P(('dom', 'outer')), may hold values from -1 to 511, as said below
Outputs:
- galerkin_rows: bfloat16 [16384, 4096], P(('dom', 'outer'))
- reduced: float32 [64, 64], replicated
Inputs may be any that keep to these rules, and one draw needn't show every extreme that they name: `ghost_rows`: each list has 4 entries, repeats allowed. `column_slot`: slot 0 holds the block row's diagonal block. Slots 0 to 3 are always used, and over the rows of one device they name every table entry exactly once. Slots 4 to 6 may be unused (-1); unused slots come after all used ones; some rows use all 7 slots and some only four.
All inputs are finite; a program needn't handle non-finite values.
Results may differ from a plain program's by a relative error of at most 0.003.
Values may be sent and summed in bfloat16 or wider, within the bound.
No kernel may reach another device: no remote copies, remote signals or barrier semaphores. Data moves between devices by JAX's collectives and lax.ppermute only.
A program may use at most 128 MiB of HBM per device.

v0:
```python
import math

import jax
import jax.numpy as jnp
from jax import lax
from jax.experimental import pallas as pl
from jax.experimental.pallas import tpu as pltpu
from jax.sharding import PartitionSpec as P

BLOCK = 64
MODES = 64
SLOTS = 7
ROW_TILE = 16


def gather_outgoing(pod_basis, picks):
    rows_local, block_area = pod_basis.shape
    count = picks.shape[0]
    sub = block_area // 128

    def body(pick_ref, pod_ref, out_ref, slab_ref):
        slab_ref[...] = pod_ref[...].reshape(rows_local, sub, 128)

        def one(n, carry):
            out_ref[n] = slab_ref[pick_ref[n]]
            return carry

        lax.fori_loop(0, count, one, 0)

    grid_spec = pltpu.PrefetchScalarGridSpec(
        num_scalar_prefetch=1,
        grid=(1,),
        in_specs=[pl.BlockSpec((rows_local, block_area), lambda i, p: (0, 0))],
        out_specs=pl.BlockSpec((count, sub, 128), lambda i, p: (0, 0, 0)),
        scratch_shapes=[pltpu.VMEM((rows_local, sub, 128), pod_basis.dtype)],
    )
    return pl.pallas_call(
        body,
        grid_spec=grid_spec,
        out_shape=jax.ShapeDtypeStruct((count, sub, 128), pod_basis.dtype),
    )(picks, pod_basis)


def block_products(jac_by_slot, table, column_slot):
    slots, rows, block_area = jac_by_slot.shape
    entries = table.shape[0]
    tile = ROW_TILE
    flat_slots = column_slot.reshape(-1)

    def body(col_ref, jac_ref, tab_ref, out_ref, part_ref):
        step = pl.program_id(0)
        acc = jnp.zeros((tile, BLOCK, MODES), jnp.float32)
        diag = None
        for j in range(slots):
            lhs = jac_ref[j].reshape(tile, BLOCK, BLOCK)
            picked = []
            for r in range(tile):
                e = col_ref[(step * tile + r) * slots + j]
                blk = tab_ref[jnp.maximum(e, 0)]
                picked.append(jnp.where(e >= 0, blk, jnp.zeros_like(blk)))
            rhs = jnp.stack(picked).reshape(tile, BLOCK, MODES)
            if j == 0:
                diag = rhs
            acc = acc + jnp.einsum(
                "rik,rkm->rim", lhs, rhs, preferred_element_type=jnp.float32
            )
        rounded = acc.astype(jnp.bfloat16)
        out_ref[...] = rounded.reshape(tile, block_area)
        contrib = lax.dot_general(
            diag.reshape(tile * BLOCK, MODES),
            rounded.reshape(tile * BLOCK, MODES),
            (((0,), (0,)), ((), ())),
            preferred_element_type=jnp.float32,
        )

        @pl.when(step == 0)
        def _():
            part_ref[...] = jnp.zeros_like(part_ref)

        part_ref[...] += contrib

    grid_spec = pltpu.PrefetchScalarGridSpec(
        num_scalar_prefetch=1,
        grid=(rows // tile,),
        in_specs=[
            pl.BlockSpec((slots, tile, block_area), lambda i, c: (0, i, 0)),
            pl.BlockSpec(table.shape, lambda i, c: (0, 0, 0)),
        ],
        out_specs=[
            pl.BlockSpec((tile, block_area), lambda i, c: (i, 0)),
            pl.BlockSpec((MODES, MODES), lambda i, c: (0, 0)),
        ],
    )
    return pl.pallas_call(
        body,
        grid_spec=grid_spec,
        out_shape=(
            jax.ShapeDtypeStruct((rows, block_area), jnp.bfloat16),
            jax.ShapeDtypeStruct((MODES, MODES), jnp.float32),
        ),
        compiler_params=pltpu.CompilerParams(dimension_semantics=("arbitrary",)),
    )(flat_slots, jac_by_slot, table)


def on_device(jacobian, pod_basis, ghost_rows, column_slot):
    rows_local = pod_basis.shape[0]
    dom_count = lax.axis_size("dom")
    outer_count = lax.axis_size("outer")
    device_count = dom_count * outer_count
    ghost_lists = ghost_rows[:, 0, :]
    ghost_count = ghost_lists.shape[1]
    outgoing = gather_outgoing(pod_basis, ghost_lists.reshape(-1))
    outgoing = outgoing.reshape((device_count, ghost_count) + outgoing.shape[1:])
    received = lax.all_to_all(outgoing, ("dom", "outer"), split_axis=0, concat_axis=0, tiled=True)
    table = received.reshape((device_count * ghost_count,) + received.shape[2:])
    jac_by_slot = jnp.transpose(jacobian, (1, 0, 2))
    galerkin_rows, partial_value = block_products(jac_by_slot, table, column_slot)
    total = partial_value
    for bit in range(device_count.bit_length() - 1):
        pairs = [(i, i ^ (1 << bit)) for i in range(device_count)]
        total = total + lax.ppermute(total, ("dom", "outer"), pairs)
    reduced = total / math.sqrt(rows_local * device_count * BLOCK)
    return (galerkin_rows, reduced)


def solution(mesh):
    placed = (
        P(("dom", "outer"), None, None),
        P(("dom", "outer"), None),
        P(None, ("dom", "outer"), None),
        P(("dom", "outer"), None),
    )
    return jax.shard_map(
        on_device,
        mesh=mesh,
        in_specs=placed,
        out_specs=(P(("dom", "outer"), None), P()),
        check_vma=False,
    )
```

profile of v0, /device:TPU:0, one launch (start us, length us, event | category | flops | bytes accessed | tf_op | source)
XLA Modules:
  0.0 144.9 jit_solution(13833990645407205880)
XLA Ops:
  0.6 0.8 copy.7
  1.4 0.7 reshape_squeeze.3.pick_ref
  2.1 7.6 %shard_map.59 = bf16[512,32,128]{2,1,0:T(8,128)(2,1)} custom-call(s32[512]{0:T(512)} %reshape_squeeze.3.pick_ref, bf16[128,4096]{1,0:T(8,128)(2,1)} %pod_ref.1), custom_call_target="tpu_custom_call" | custom-call | tf_op jit(solution)/shard_map/pallas_call | solution.py:37
  9.8 0.0 copy-start
  9.8 11.7 %all-to-all-start = ((bf16[128,4,32,128]{3,2,1,0:T(8,128)(2,1)}), bf16[128,4,32,128]{3,2,1,0:T(8,128)(2,1)}, u32[]{:S(2)}, u32[]{:S(2)}) async-start(bf16[128,4,32,128]{3,2,1,0:T(8,128)(2,1)} %bitcast.5), calls=%async_computation | async-start | bytes 8388608 | tf_op jit(solution)/shard_map/all_to_all | solution.py:114
  21.5 0.0 copy-done
  21.5 0.1 copy.6
  21.6 0.8 reshape.13.col_ref
  22.4 51.6 %all-to-all-done = bf16[128,4,32,128]{3,2,1,0:T(8,128)(2,1)} async-done(((bf16[128,4,32,128]{3,2,1,0:T(8,128)(2,1)}), bf16[128,4,32,128]{3,2,1,0:T(8,128)(2,1)}, u32[]{:S(2)}, u32[]{:S(2)}) %all-to-all-start) | async-done | bytes 4194336 | tf_op jit(solution)/shard_map/all_to_all | solution.py:114
  74.0 40.0 %shard_map.60 = (bf16[128,4096]{1,0:T(8,128)(2,1)}, f32[64,64]{1,0:T(8,128)}) custom-call(s32[896]{0:T(1024)} %reshape.13.col_ref, bf16[7,128,4096]{2,1,0:T(8,128)(2,1)} %bitcast.6, bf16[512,32,128]{2,1,0:T(8,128)(2,1)} %bitcast.2.tab_ref), custom_call_target="tpu_custom_call" | custom-call | tf_op jit(solution)/shard_map/pallas_call | solution.py:94
  114.1 0.0 collective-permute-start
  114.1 1.4 collective-permute-done
  115.5 0.8 add.21
  116.3 0.4 collective-permute-start.1
  116.7 3.5 %collective-permute-done.1 = f32[64,64]{1,0:T(8,128)S(1)} collective-permute-done((f32[64,64]{1,0:T(8,128)S(1)}, f32[64,64]{1,0:T(8,128)S(1)}, u32[]{:S(2)}, u32[]{:S(2)}) %collective-permute-start.1) | collective-permute-done | bytes 16416 | tf_op jit(solution)/shard_map/ppermute | solution.py:121
  120.2 0.6 collective-permute-start.2
  120.7 4.9 %collective-permute-done.2 = f32[64,64]{1,0:T(8,128)S(1)} collective-permute-done((f32[64,64]{1,0:T(8,128)S(1)}, f32[64,64]{1,0:T(8,128)S(1)}, u32[]{:S(2)}, u32[]{:S(2)}) %collective-permute-start.2) | collective-permute-done | bytes 16416 | tf_op jit(solution)/shard_map/ppermute | solution.py:121
  125.6 0.6 collective-permute-start.3
  126.2 3.3 %collective-permute-done.3 = f32[64,64]{1,0:T(8,128)S(1)} collective-permute-done((f32[64,64]{1,0:T(8,128)S(1)}, f32[64,64]{1,0:T(8,128)S(1)}, u32[]{:S(2)}, u32[]{:S(2)}) %collective-permute-start.3) | collective-permute-done | bytes 16416 | tf_op jit(solution)/shard_map/ppermute | solution.py:121
  129.5 0.8 collective-permute-start.4
  130.4 4.6 %collective-permute-done.4 = f32[64,64]{1,0:T(8,128)S(1)} collective-permute-done((f32[64,64]{1,0:T(8,128)S(1)}, f32[64,64]{1,0:T(8,128)S(1)}, u32[]{:S(2)}, u32[]{:S(2)}) %collective-permute-start.4) | collective-permute-done | bytes 16416 | tf_op jit(solution)/shard_map/ppermute | solution.py:121
  134.9 0.5 collective-permute-start.5
  135.5 3.4 %collective-permute-done.5 = f32[64,64]{1,0:T(8,128)S(1)} collective-permute-done((f32[64,64]{1,0:T(8,128)S(1)}, f32[64,64]{1,0:T(8,128)S(1)}, u32[]{:S(2)}, u32[]{:S(2)}) %collective-permute-start.5) | collective-permute-done | bytes 16416 | tf_op jit(solution)/shard_map/ppermute | solution.py:121
  138.9 1.9 %collective-permute-start.6 = (f32[64,64]{1,0:T(8,128)S(1)}, f32[64,64]{1,0:T(8,128)S(1)}, u32[]{:S(2)}, u32[]{:S(2)}) collective-permute-start(f32[64,64]{1,0:T(8,128)S(1)} %add.26), channel_id=1, source_target_pairs={{0,64},{1,65},{2,66},{3,67},{4,68},{5,69},{6,70},{7,71},{8,72},{9,... | collective-permute-start | bytes 49160 | tf_op jit(solution)/shard_map/ppermute | solution.py:121
  140.7 3.6 %collective-permute-done.6 = f32[64,64]{1,0:T(8,128)S(1)} collective-permute-done((f32[64,64]{1,0:T(8,128)S(1)}, f32[64,64]{1,0:T(8,128)S(1)}, u32[]{:S(2)}, u32[]{:S(2)}) %collective-permute-start.6) | collective-permute-done | bytes 16416 | tf_op jit(solution)/shard_map/ppermute | solution.py:121
  144.3 0.6 add_multiply_fusion
  (5 shorter events, 0.0 us)
Async XLA Ops:
  9.8 11.7 %copy-start = (s32[128,7]{0,1:T(8,128)S(1)}, s32[128,7]{0,1:T(8,128)}, u32[]{:S(2)}) copy-start(s32[128,7]{0,1:T(8,128)} %param.7) | copy-start | bytes 10756
  9.8 64.3 %all-to-all-start = ((bf16[128,4,32,128]{3,2,1,0:T(8,128)(2,1)}), bf16[128,4,32,128]{3,2,1,0:T(8,128)(2,1)}, u32[]{:S(2)}, u32[]{:S(2)}) async-start(bf16[128,4,32,128]{3,2,1,0:T(8,128)(2,1)} %bitcast.5), calls=%async_computation | async-start | bytes 8388608 | tf_op jit(solution)/shard_map/all_to_all | solution.py:114
  114.1 1.4 collective-permute-start
  116.3 3.9 %collective-permute-start.1 = (f32[64,64]{1,0:T(8,128)S(1)}, f32[64,64]{1,0:T(8,128)S(1)}, u32[]{:S(2)}, u32[]{:S(2)}) collective-permute-start(f32[64,64]{1,0:T(8,128)S(1)} %add.21), channel_id=1, source_target_pairs={{0,2},{1,3},{2,0},{3,1},{4,6},{5,7},{6,4},{7,5},{8,10},{9,11},{10,... | collective-permute-start | bytes 49160 | tf_op jit(solution)/shard_map/ppermute | solution.py:121
  120.2 5.4 %collective-permute-start.2 = (f32[64,64]{1,0:T(8,128)S(1)}, f32[64,64]{1,0:T(8,128)S(1)}, u32[]{:S(2)}, u32[]{:S(2)}) collective-permute-start(f32[64,64]{1,0:T(8,128)S(1)} %add.22), channel_id=1, source_target_pairs={{0,4},{1,5},{2,6},{3,7},{4,0},{5,1},{6,2},{7,3},{8,12},{9,13},{10,... | collective-permute-start | bytes 49160 | tf_op jit(solution)/shard_map/ppermute | solution.py:121
  125.6 3.9 %collective-permute-start.3 = (f32[64,64]{1,0:T(8,128)S(1)}, f32[64,64]{1,0:T(8,128)S(1)}, u32[]{:S(2)}, u32[]{:S(2)}) collective-permute-start(f32[64,64]{1,0:T(8,128)S(1)} %add.23), channel_id=1, source_target_pairs={{0,8},{1,9},{2,10},{3,11},{4,12},{5,13},{6,14},{7,15},{8,0},{9,1},... | collective-permute-start | bytes 49160 | tf_op jit(solution)/shard_map/ppermute | solution.py:121
  129.5 5.4 %collective-permute-start.4 = (f32[64,64]{1,0:T(8,128)S(1)}, f32[64,64]{1,0:T(8,128)S(1)}, u32[]{:S(2)}, u32[]{:S(2)}) collective-permute-start(f32[64,64]{1,0:T(8,128)S(1)} %add.24), channel_id=1, source_target_pairs={{0,16},{1,17},{2,18},{3,19},{4,20},{5,21},{6,22},{7,23},{8,24},{9,... | collective-permute-start | bytes 49160 | tf_op jit(solution)/shard_map/ppermute | solution.py:121
  134.9 3.9 %collective-permute-start.5 = (f32[64,64]{1,0:T(8,128)S(1)}, f32[64,64]{1,0:T(8,128)S(1)}, u32[]{:S(2)}, u32[]{:S(2)}) collective-permute-start(f32[64,64]{1,0:T(8,128)S(1)} %add.25), channel_id=1, source_target_pairs={{0,32},{1,33},{2,34},{3,35},{4,36},{5,37},{6,38},{7,39},{8,40},{9,... | collective-permute-start | bytes 49160 | tf_op jit(solution)/shard_map/ppermute | solution.py:121
  138.9 5.4 %collective-permute-start.6 = (f32[64,64]{1,0:T(8,128)S(1)}, f32[64,64]{1,0:T(8,128)S(1)}, u32[]{:S(2)}, u32[]{:S(2)}) collective-permute-start(f32[64,64]{1,0:T(8,128)S(1)} %add.26), channel_id=1, source_target_pairs={{0,64},{1,65},{2,66},{3,67},{4,68},{5,69},{6,70},{7,71},{8,72},{9,... | collective-permute-start | bytes 49160 | tf_op jit(solution)/shard_map/ppermute | solution.py:121
where the time goes:
time: 145 us
  waiting for transfers between devices  76.3 us (53%)
  Pallas kernels  47.7 us (33%)
  starting transfers between devices  16.4 us (11%)
  local copies, waits for them, and re-layouts  2.39 us (2%)
    all_to_all x1, waiting for transfers between devices, on_device(): lax.all_to_all(outgoing, ('dom', 'outer'), split_axis=0, concat_axis=0, t...  51.6 us
    pallas_call x1, Pallas kernels, block_products(): pl.pallas_call(body, grid_spec=grid_spec, out_shape=(jax.ShapeDtypeStruct...  40 us
    ppermute x7, waiting for transfers between devices, on_device(): total = total + lax.ppermute(total, ('dom', 'outer'), pairs)  24.7 us
    all_to_all x1, starting transfers between devices, on_device(): lax.all_to_all(outgoing, ('dom', 'outer'), split_axis=0, concat_axis=0, t...  11.7 us
    pallas_call x1, Pallas kernels, gather_outgoing(): pl.pallas_call(body, grid_spec=grid_spec, out_shape=jax.ShapeDtypeStruct(...  7.65 us
    ppermute x7, starting transfers between devices, on_device(): total = total + lax.ppermute(total, ('dom', 'outer'), pairs)  4.74 us
  transfers between devices with their start and end apart: 8, of which 8 were waited for; matrix products, arithmetic and copies ran while one was open for 1% of the time, Pallas kernels for 0%

commit v1 on v0

--- a/solution.py
+++ b/solution.py
@@ -25,7 +25,7 @@
             out_ref[n] = slab_ref[pick_ref[n]]
             return carry
 
-        lax.fori_loop(0, count, one, 0)
+        lax.fori_loop(0, count, one, 0, unroll=8)
 
     grid_spec = pltpu.PrefetchScalarGridSpec(
         num_scalar_prefetch=1,
@@ -47,8 +47,20 @@
     tile = ROW_TILE
     flat_slots = column_slot.reshape(-1)
 
-    def body(col_ref, jac_ref, tab_ref, out_ref, part_ref):
+    def body(col_ref, jac_ref, tab_ref, out_ref, part_ref, blocks_ref):
         step = pl.program_id(0)
+
+        @pl.when(step == 0)
+        def _():
+            def relayout(c, carry):
+                chunk = pl.ds(c * tile, tile)
+                blocks_ref[chunk] = tab_ref[chunk].reshape(tile, BLOCK, MODES)
+                return carry
+
+            lax.fori_loop(0, entries // tile, relayout, 0)
+            blocks_ref[entries] = jnp.zeros((BLOCK, MODES), blocks_ref.dtype)
+            part_ref[...] = jnp.zeros_like(part_ref)
+
         acc = jnp.zeros((tile, BLOCK, MODES), jnp.float32)
         diag = None
         for j in range(slots):
@@ -56,9 +68,8 @@
             picked = []
             for r in range(tile):
                 e = col_ref[(step * tile + r) * slots + j]
-                blk = tab_ref[jnp.maximum(e, 0)]
-                picked.append(jnp.where(e >= 0, blk, jnp.zeros_like(blk)))
-            rhs = jnp.stack(picked).reshape(tile, BLOCK, MODES)
+                picked.append(blocks_ref[jnp.where(e >= 0, e, entries)])
+            rhs = jnp.stack(picked)
             if j == 0:
                 diag = rhs
             acc = acc + jnp.einsum(
@@ -66,18 +77,12 @@
             )
         rounded = acc.astype(jnp.bfloat16)
         out_ref[...] = rounded.reshape(tile, block_area)
-        contrib = lax.dot_general(
+        part_ref[...] += lax.dot_general(
             diag.reshape(tile * BLOCK, MODES),
             rounded.reshape(tile * BLOCK, MODES),
             (((0,), (0,)), ((), ())),
             preferred_element_type=jnp.float32,
         )
-
-        @pl.when(step == 0)
-        def _():
-            part_ref[...] = jnp.zeros_like(part_ref)
-
-        part_ref[...] += contrib
 
     grid_spec = pltpu.PrefetchScalarGridSpec(
         num_scalar_prefetch=1,
@@ -90,6 +95,7 @@
             pl.BlockSpec((tile, block_area), lambda i, c: (i, 0)),
             pl.BlockSpec((MODES, MODES), lambda i, c: (0, 0)),
         ],
+        scratch_shapes=[pltpu.VMEM((entries + 1, BLOCK, MODES), table.dtype)],
     )
     return pl.pallas_call(
         body,

time: 145 us -> 135 us (0.931)
  Pallas kernels: 47.7 us -> 37.5 us
    pallas_call x1, Pallas kernels: 40 us -> 32.2 us  [block_products(): pl.pallas_call(body, grid_spec=grid_spec, out_shape=(jax.ShapeDtypeStruct...]
    pallas_call x1, Pallas kernels: 7.65 us -> 5.29 us  [gather_outgoing(): pl.pallas_call(body, grid_spec=grid_spec, out_shape=jax.ShapeDtypeStruct(...]
where the time goes in v1:
time: 135 us
  waiting for transfers between devices  76.3 us (57%)
  Pallas kernels  37.5 us (28%)
  starting transfers between devices  16.4 us (12%)
  local copies, waits for them, and re-layouts  2.39 us (2%)
  other arithmetic  1.41 us (1%)
    all_to_all x1, waiting for transfers between devices, on_device(): lax.all_to_all(outgoing, ('dom', 'outer'), split_axis=0, concat_axis=0, t...  51.6 us
    pallas_call x1, Pallas kernels, block_products(): pl.pallas_call(body, grid_spec=grid_spec, out_shape=(jax.ShapeDtypeStruct...  32.2 us
    ppermute x7, waiting for transfers between devices, on_device(): total = total + lax.ppermute(total, ('dom', 'outer'), pairs)  24.7 us
    all_to_all x1, starting transfers between devices, on_device(): lax.all_to_all(outgoing, ('dom', 'outer'), split_axis=0, concat_axis=0, t...  11.7 us
    pallas_call x1, Pallas kernels, gather_outgoing(): pl.pallas_call(body, grid_spec=grid_spec, out_shape=jax.ShapeDtypeStruct(...  5.29 us
    ppermute x7, starting transfers between devices, on_device(): total = total + lax.ppermute(total, ('dom', 'outer'), pairs)  4.73 us
  transfers between devices with their start and end apart: 8, of which 8 were waited for; matrix products, arithmetic and copies ran while one was open for 1% of the time, Pallas kernels for 0%

profile of v1, /device:TPU:0, one launch (start us, length us, event | category | flops | bytes accessed | tf_op | source)
XLA Modules:
  0.0 134.8 jit_solution(17192833010730830918)
XLA Ops:
  0.6 0.8 copy.7
  1.4 0.7 reshape_squeeze.3.pick_ref
  2.1 5.3 %shard_map.59 = bf16[512,32,128]{2,1,0:T(8,128)(2,1)} custom-call(s32[512]{0:T(512)} %reshape_squeeze.3.pick_ref, bf16[128,4096]{1,0:T(8,128)(2,1)} %pod_ref.1), custom_call_target="tpu_custom_call" | custom-call | tf_op jit(solution)/shard_map/pallas_call | solution.py:37
  7.4 0.0 copy-start
  7.4 11.7 %all-to-all-start = ((bf16[128,4,32,128]{3,2,1,0:T(8,128)(2,1)}), bf16[128,4,32,128]{3,2,1,0:T(8,128)(2,1)}, u32[]{:S(2)}, u32[]{:S(2)}) async-start(bf16[128,4,32,128]{3,2,1,0:T(8,128)(2,1)} %bitcast.5), calls=%async_computation | async-start | bytes 8388608 | tf_op jit(solution)/shard_map/all_to_all | solution.py:120
  19.1 0.0 copy-done
  19.1 0.1 copy.6
  19.2 0.8 reshape.13.col_ref
  20.0 51.6 %all-to-all-done = bf16[128,4,32,128]{3,2,1,0:T(8,128)(2,1)} async-done(((bf16[128,4,32,128]{3,2,1,0:T(8,128)(2,1)}), bf16[128,4,32,128]{3,2,1,0:T(8,128)(2,1)}, u32[]{:S(2)}, u32[]{:S(2)}) %all-to-all-start) | async-done | bytes 4194336 | tf_op jit(solution)/shard_map/all_to_all | solution.py:120
  71.7 32.2 %shard_map.60 = (bf16[128,4096]{1,0:T(8,128)(2,1)}, f32[64,64]{1,0:T(8,128)}) custom-call(s32[896]{0:T(1024)} %reshape.13.col_ref, bf16[7,128,4096]{2,1,0:T(8,128)(2,1)} %bitcast.6, bf16[512,32,128]{2,1,0:T(8,128)(2,1)} %bitcast.2.tab_ref), custom_call_target="tpu_custom_call" | custom-call | tf_op jit(solution)/shard_map/pallas_call | solution.py:100
  103.9 0.0 collective-permute-start
  103.9 1.4 %collective-permute-done = f32[64,64]{1,0:T(8,128)S(1)} collective-permute-done((f32[64,64]{1,0:T(8,128)}, f32[64,64]{1,0:T(8,128)S(1)}, u32[]{:S(2)}, u32[]{:S(2)}) %collective-permute-start) | collective-permute-done | bytes 16416 | tf_op jit(solution)/shard_map/ppermute | solution.py:127
  105.3 0.8 add.21
  106.1 0.4 collective-permute-start.1
  106.5 3.5 %collective-permute-done.1 = f32[64,64]{1,0:T(8,128)S(1)} collective-permute-done((f32[64,64]{1,0:T(8,128)S(1)}, f32[64,64]{1,0:T(8,128)S(1)}, u32[]{:S(2)}, u32[]{:S(2)}) %collective-permute-start.1) | collective-permute-done | bytes 16416 | tf_op jit(solution)/shard_map/ppermute | solution.py:127
  110.0 0.6 collective-permute-start.2
  110.6 4.9 %collective-permute-done.2 = f32[64,64]{1,0:T(8,128)S(1)} collective-permute-done((f32[64,64]{1,0:T(8,128)S(1)}, f32[64,64]{1,0:T(8,128)S(1)}, u32[]{:S(2)}, u32[]{:S(2)}) %collective-permute-start.2) | collective-permute-done | bytes 16416 | tf_op jit(solution)/shard_map/ppermute | solution.py:127
  115.4 0.6 collective-permute-start.3
  116.0 3.4 %collective-permute-done.3 = f32[64,64]{1,0:T(8,128)S(1)} collective-permute-done((f32[64,64]{1,0:T(8,128)S(1)}, f32[64,64]{1,0:T(8,128)S(1)}, u32[]{:S(2)}, u32[]{:S(2)}) %collective-permute-start.3) | collective-permute-done | bytes 16416 | tf_op jit(solution)/shard_map/ppermute | solution.py:127
  119.4 0.8 collective-permute-start.4
  120.2 4.6 %collective-permute-done.4 = f32[64,64]{1,0:T(8,128)S(1)} collective-permute-done((f32[64,64]{1,0:T(8,128)S(1)}, f32[64,64]{1,0:T(8,128)S(1)}, u32[]{:S(2)}, u32[]{:S(2)}) %collective-permute-start.4) | collective-permute-done | bytes 16416 | tf_op jit(solution)/shard_map/ppermute | solution.py:127
  124.8 0.5 collective-permute-start.5
  125.3 3.4 %collective-permute-done.5 = f32[64,64]{1,0:T(8,128)S(1)} collective-permute-done((f32[64,64]{1,0:T(8,128)S(1)}, f32[64,64]{1,0:T(8,128)S(1)}, u32[]{:S(2)}, u32[]{:S(2)}) %collective-permute-start.5) | collective-permute-done | bytes 16416 | tf_op jit(solution)/shard_map/ppermute | solution.py:127
  128.7 1.9 %collective-permute-start.6 = (f32[64,64]{1,0:T(8,128)S(1)}, f32[64,64]{1,0:T(8,128)S(1)}, u32[]{:S(2)}, u32[]{:S(2)}) collective-permute-start(f32[64,64]{1,0:T(8,128)S(1)} %add.26), channel_id=1, source_target_pairs={{0,64},{1,65},{2,66},{3,67},{4,68},{5,69},{6,70},{7,71},{8,72},{9,... | collective-permute-start | bytes 49160 | tf_op jit(solution)/shard_map/ppermute | solution.py:127
  130.6 3.6 %collective-permute-done.6 = f32[64,64]{1,0:T(8,128)S(1)} collective-permute-done((f32[64,64]{1,0:T(8,128)S(1)}, f32[64,64]{1,0:T(8,128)S(1)}, u32[]{:S(2)}, u32[]{:S(2)}) %collective-permute-start.6) | collective-permute-done | bytes 16416 | tf_op jit(solution)/shard_map/ppermute | solution.py:127
  134.1 0.6 add_multiply_fusion
  (5 shorter events, 0.0 us)
Async XLA Ops:
  7.4 11.7 %copy-start = (s32[128,7]{0,1:T(8,128)S(1)}, s32[128,7]{0,1:T(8,128)}, u32[]{:S(2)}) copy-start(s32[128,7]{0,1:T(8,128)} %param.7) | copy-start | bytes 10756
  7.4 64.3 %all-to-all-start = ((bf16[128,4,32,128]{3,2,1,0:T(8,128)(2,1)}), bf16[128,4,32,128]{3,2,1,0:T(8,128)(2,1)}, u32[]{:S(2)}, u32[]{:S(2)}) async-start(bf16[128,4,32,128]{3,2,1,0:T(8,128)(2,1)} %bitcast.5), calls=%async_computation | async-start | bytes 8388608 | tf_op jit(solution)/shard_map/all_to_all | solution.py:120
  103.9 1.4 %collective-permute-start = (f32[64,64]{1,0:T(8,128)}, f32[64,64]{1,0:T(8,128)S(1)}, u32[]{:S(2)}, u32[]{:S(2)}) collective-permute-start(f32[64,64]{1,0:T(8,128)} %get-tuple-element.5), channel_id=1, source_target_pairs={{0,1},{1,0},{2,3},{3,2},{4,5},{5,4},{6,7},{7,6},{8,9},{9,8},{10,11... | collective-permute-start | bytes 49160 | tf_op jit(solution)/shard_map/ppermute | solution.py:127
  106.1 3.9 %collective-permute-start.1 = (f32[64,64]{1,0:T(8,128)S(1)}, f32[64,64]{1,0:T(8,128)S(1)}, u32[]{:S(2)}, u32[]{:S(2)}) collective-permute-start(f32[64,64]{1,0:T(8,128)S(1)} %add.21), channel_id=1, source_target_pairs={{0,2},{1,3},{2,0},{3,1},{4,6},{5,7},{6,4},{7,5},{8,10},{9,11},{10,... | collective-permute-start | bytes 49160 | tf_op jit(solution)/shard_map/ppermute | solution.py:127
  110.0 5.4 %collective-permute-start.2 = (f32[64,64]{1,0:T(8,128)S(1)}, f32[64,64]{1,0:T(8,128)S(1)}, u32[]{:S(2)}, u32[]{:S(2)}) collective-permute-start(f32[64,64]{1,0:T(8,128)S(1)} %add.22), channel_id=1, source_target_pairs={{0,4},{1,5},{2,6},{3,7},{4,0},{5,1},{6,2},{7,3},{8,12},{9,13},{10,... | collective-permute-start | bytes 49160 | tf_op jit(solution)/shard_map/ppermute | solution.py:127
  115.4 3.9 %collective-permute-start.3 = (f32[64,64]{1,0:T(8,128)S(1)}, f32[64,64]{1,0:T(8,128)S(1)}, u32[]{:S(2)}, u32[]{:S(2)}) collective-permute-start(f32[64,64]{1,0:T(8,128)S(1)} %add.23), channel_id=1, source_target_pairs={{0,8},{1,9},{2,10},{3,11},{4,12},{5,13},{6,14},{7,15},{8,0},{9,1},... | collective-permute-start | bytes 49160 | tf_op jit(solution)/shard_map/ppermute | solution.py:127
  119.4 5.4 %collective-permute-start.4 = (f32[64,64]{1,0:T(8,128)S(1)}, f32[64,64]{1,0:T(8,128)S(1)}, u32[]{:S(2)}, u32[]{:S(2)}) collective-permute-start(f32[64,64]{1,0:T(8,128)S(1)} %add.24), channel_id=1, source_target_pairs={{0,16},{1,17},{2,18},{3,19},{4,20},{5,21},{6,22},{7,23},{8,24},{9,... | collective-permute-start | bytes 49160 | tf_op jit(solution)/shard_map/ppermute | solution.py:127
  124.8 3.9 %collective-permute-start.5 = (f32[64,64]{1,0:T(8,128)S(1)}, f32[64,64]{1,0:T(8,128)S(1)}, u32[]{:S(2)}, u32[]{:S(2)}) collective-permute-start(f32[64,64]{1,0:T(8,128)S(1)} %add.25), channel_id=1, source_target_pairs={{0,32},{1,33},{2,34},{3,35},{4,36},{5,37},{6,38},{7,39},{8,40},{9,... | collective-permute-start | bytes 49160 | tf_op jit(solution)/shard_map/ppermute | solution.py:127
  128.7 5.4 %collective-permute-start.6 = (f32[64,64]{1,0:T(8,128)S(1)}, f32[64,64]{1,0:T(8,128)S(1)}, u32[]{:S(2)}, u32[]{:S(2)}) collective-permute-start(f32[64,64]{1,0:T(8,128)S(1)} %add.26), channel_id=1, source_target_pairs={{0,64},{1,65},{2,66},{3,67},{4,68},{5,69},{6,70},{7,71},{8,72},{9,... | collective-permute-start | bytes 49160 | tf_op jit(solution)/shard_map/ppermute | solution.py:127

commit v2 on v1

--- a/solution.py
+++ b/solution.py
@@ -10,7 +10,8 @@
 BLOCK = 64
 MODES = 64
 SLOTS = 7
-ROW_TILE = 16
+ROW_TILE = 32
+SEND_STEPS = 4
 
 
 def gather_outgoing(pod_basis, picks):
@@ -18,26 +19,33 @@
     count = picks.shape[0]
     sub = block_area // 128
 
+    per_step = count // SEND_STEPS
+
     def body(pick_ref, pod_ref, out_ref, slab_ref):
-        slab_ref[...] = pod_ref[...].reshape(rows_local, sub, 128)
+        step = pl.program_id(0)
+
+        @pl.when(step == 0)
+        def _():
+            slab_ref[...] = pod_ref[...].reshape(rows_local, sub, 128)
 
         def one(n, carry):
-            out_ref[n] = slab_ref[pick_ref[n]]
+            out_ref[n] = slab_ref[pick_ref[step * per_step + n]]
             return carry
 
-        lax.fori_loop(0, count, one, 0, unroll=8)
+        lax.fori_loop(0, per_step, one, 0, unroll=8)
 
     grid_spec = pltpu.PrefetchScalarGridSpec(
         num_scalar_prefetch=1,
-        grid=(1,),
+        grid=(SEND_STEPS,),
         in_specs=[pl.BlockSpec((rows_local, block_area), lambda i, p: (0, 0))],
-        out_specs=pl.BlockSpec((count, sub, 128), lambda i, p: (0, 0, 0)),
+        out_specs=pl.BlockSpec((per_step, sub, 128), lambda i, p: (i, 0, 0)),
         scratch_shapes=[pltpu.VMEM((rows_local, sub, 128), pod_basis.dtype)],
     )
     return pl.pallas_call(
         body,
         grid_spec=grid_spec,
         out_shape=jax.ShapeDtypeStruct((count, sub, 128), pod_basis.dtype),
+        compiler_params=pltpu.CompilerParams(dimension_semantics=("arbitrary",)),
     )(picks, pod_basis)
 
 

time: 135 us -> 133 us (0.985)
  Pallas kernels: 37.5 us -> 35 us
    pallas_call x1, Pallas kernels: 32.2 us -> 29.7 us  [block_products(): pl.pallas_call(body, grid_spec=grid_spec, out_shape=(jax.ShapeDtypeStruct...]
where the time goes in v2:
time: 133 us; the launch traced here: 132 us
  waiting for transfers between devices  76.3 us (57%)
  Pallas kernels  35 us (26%)
  starting transfers between devices  16.4 us (12%)
  local copies, waits for them, and re-layouts  2.39 us (2%)
  other arithmetic  1.41 us (1%)
    all_to_all x1, waiting for transfers between devices, on_device(): lax.all_to_all(outgoing, ('dom', 'outer'), split_axis=0, concat_axis=0, t...  51.6 us
    pallas_call x1, Pallas kernels, block_products(): pl.pallas_call(body, grid_spec=grid_spec, out_shape=(jax.ShapeDtypeStruct...  29.7 us
    ppermute x7, waiting for transfers between devices, on_device(): total = total + lax.ppermute(total, ('dom', 'outer'), pairs)  24.7 us
    all_to_all x1, starting transfers between devices, on_device(): lax.all_to_all(outgoing, ('dom', 'outer'), split_axis=0, concat_axis=0, t...  11.7 us
    pallas_call x1, Pallas kernels, gather_outgoing(): pl.pallas_call(body, grid_spec=grid_spec, out_shape=jax.ShapeDtypeStruct(...  5.31 us
    ppermute x7, starting transfers between devices, on_device(): total = total + lax.ppermute(total, ('dom', 'outer'), pairs)  4.74 us
  transfers between devices with their start and end apart: 8, of which 8 were waited for; matrix products, arithmetic and copies ran while one was open for 1% of the time, Pallas kernels for 0%

profile of v2, /device:TPU:0, one launch (start us, length us, event | category | flops | bytes accessed | tf_op | source)
XLA Modules:
  0.0 132.2 jit_solution(11486604864732419906)
XLA Ops:
  0.6 0.8 copy.7
  1.4 0.7 reshape_squeeze.3.pick_ref
  2.1 5.3 %shard_map.59 = bf16[512,32,128]{2,1,0:T(8,128)(2,1)} custom-call(s32[512]{0:T(512)} %reshape_squeeze.3.pick_ref, bf16[128,4096]{1,0:T(8,128)(2,1)} %pod_ref.1), custom_call_target="tpu_custom_call" | custom-call | tf_op jit(solution)/shard_map/pallas_call | solution.py:44
  7.4 0.0 copy-start
  7.4 11.7 %all-to-all-start = ((bf16[128,4,32,128]{3,2,1,0:T(8,128)(2,1)}), bf16[128,4,32,128]{3,2,1,0:T(8,128)(2,1)}, u32[]{:S(2)}, u32[]{:S(2)}) async-start(bf16[128,4,32,128]{3,2,1,0:T(8,128)(2,1)} %bitcast.5), calls=%async_computation | async-start | bytes 8388608 | tf_op jit(solution)/shard_map/all_to_all | solution.py:128
  19.1 0.0 copy-done
  19.1 0.1 copy.6
  19.2 0.8 reshape.13.col_ref
  20.0 51.6 %all-to-all-done = bf16[128,4,32,128]{3,2,1,0:T(8,128)(2,1)} async-done(((bf16[128,4,32,128]{3,2,1,0:T(8,128)(2,1)}), bf16[128,4,32,128]{3,2,1,0:T(8,128)(2,1)}, u32[]{:S(2)}, u32[]{:S(2)}) %all-to-all-start) | async-done | bytes 4194336 | tf_op jit(solution)/shard_map/all_to_all | solution.py:128
  71.7 29.7 %shard_map.60 = (bf16[128,4096]{1,0:T(8,128)(2,1)}, f32[64,64]{1,0:T(8,128)}) custom-call(s32[896]{0:T(1024)} %reshape.13.col_ref, bf16[7,128,4096]{2,1,0:T(8,128)(2,1)} %bitcast.6, bf16[512,32,128]{2,1,0:T(8,128)(2,1)} %bitcast.2.tab_ref), custom_call_target="tpu_custom_call" | custom-call | tf_op jit(solution)/shard_map/pallas_call | solution.py:108
  101.4 0.0 collective-permute-start
  101.4 1.4 %collective-permute-done = f32[64,64]{1,0:T(8,128)S(1)} collective-permute-done((f32[64,64]{1,0:T(8,128)}, f32[64,64]{1,0:T(8,128)S(1)}, u32[]{:S(2)}, u32[]{:S(2)}) %collective-permute-start) | collective-permute-done | bytes 16416 | tf_op jit(solution)/shard_map/ppermute | solution.py:135
  102.8 0.8 add.21
  103.6 0.4 collective-permute-start.1
  104.0 3.5 %collective-permute-done.1 = f32[64,64]{1,0:T(8,128)S(1)} collective-permute-done((f32[64,64]{1,0:T(8,128)S(1)}, f32[64,64]{1,0:T(8,128)S(1)}, u32[]{:S(2)}, u32[]{:S(2)}) %collective-permute-start.1) | collective-permute-done | bytes 16416 | tf_op jit(solution)/shard_map/ppermute | solution.py:135
  107.5 0.6 collective-permute-start.2
  108.0 4.9 %collective-permute-done.2 = f32[64,64]{1,0:T(8,128)S(1)} collective-permute-done((f32[64,64]{1,0:T(8,128)S(1)}, f32[64,64]{1,0:T(8,128)S(1)}, u32[]{:S(2)}, u32[]{:S(2)}) %collective-permute-start.2) | collective-permute-done | bytes 16416 | tf_op jit(solution)/shard_map/ppermute | solution.py:135
  112.9 0.6 collective-permute-start.3
  113.5 3.4 %collective-permute-done.3 = f32[64,64]{1,0:T(8,128)S(1)} collective-permute-done((f32[64,64]{1,0:T(8,128)S(1)}, f32[64,64]{1,0:T(8,128)S(1)}, u32[]{:S(2)}, u32[]{:S(2)}) %collective-permute-start.3) | collective-permute-done | bytes 16416 | tf_op jit(solution)/shard_map/ppermute | solution.py:135
  116.8 0.8 collective-permute-start.4
  117.6 4.6 %collective-permute-done.4 = f32[64,64]{1,0:T(8,128)S(1)} collective-permute-done((f32[64,64]{1,0:T(8,128)S(1)}, f32[64,64]{1,0:T(8,128)S(1)}, u32[]{:S(2)}, u32[]{:S(2)}) %collective-permute-start.4) | collective-permute-done | bytes 16416 | tf_op jit(solution)/shard_map/ppermute | solution.py:135
  122.2 0.5 collective-permute-start.5
  122.8 3.4 %collective-permute-done.5 = f32[64,64]{1,0:T(8,128)S(1)} collective-permute-done((f32[64,64]{1,0:T(8,128)S(1)}, f32[64,64]{1,0:T(8,128)S(1)}, u32[]{:S(2)}, u32[]{:S(2)}) %collective-permute-start.5) | collective-permute-done | bytes 16416 | tf_op jit(solution)/shard_map/ppermute | solution.py:135
  126.2 1.9 %collective-permute-start.6 = (f32[64,64]{1,0:T(8,128)S(1)}, f32[64,64]{1,0:T(8,128)S(1)}, u32[]{:S(2)}, u32[]{:S(2)}) collective-permute-start(f32[64,64]{1,0:T(8,128)S(1)} %add.26), channel_id=1, source_target_pairs={{0,64},{1,65},{2,66},{3,67},{4,68},{5,69},{6,70},{7,71},{8,72},{9,... | collective-permute-start | bytes 49160 | tf_op jit(solution)/shard_map/ppermute | solution.py:135
  128.0 3.6 %collective-permute-done.6 = f32[64,64]{1,0:T(8,128)S(1)} collective-permute-done((f32[64,64]{1,0:T(8,128)S(1)}, f32[64,64]{1,0:T(8,128)S(1)}, u32[]{:S(2)}, u32[]{:S(2)}) %collective-permute-start.6) | collective-permute-done | bytes 16416 | tf_op jit(solution)/shard_map/ppermute | solution.py:135
  131.6 0.6 add_multiply_fusion
  (5 shorter events, 0.0 us)
Async XLA Ops:
  7.4 11.7 %copy-start = (s32[128,7]{0,1:T(8,128)S(1)}, s32[128,7]{0,1:T(8,128)}, u32[]{:S(2)}) copy-start(s32[128,7]{0,1:T(8,128)} %param.7) | copy-start | bytes 10756
  7.4 64.3 %all-to-all-start = ((bf16[128,4,32,128]{3,2,1,0:T(8,128)(2,1)}), bf16[128,4,32,128]{3,2,1,0:T(8,128)(2,1)}, u32[]{:S(2)}, u32[]{:S(2)}) async-start(bf16[128,4,32,128]{3,2,1,0:T(8,128)(2,1)} %bitcast.5), calls=%async_computation | async-start | bytes 8388608 | tf_op jit(solution)/shard_map/all_to_all | solution.py:128
  101.4 1.4 %collective-permute-start = (f32[64,64]{1,0:T(8,128)}, f32[64,64]{1,0:T(8,128)S(1)}, u32[]{:S(2)}, u32[]{:S(2)}) collective-permute-start(f32[64,64]{1,0:T(8,128)} %get-tuple-element.5), channel_id=1, source_target_pairs={{0,1},{1,0},{2,3},{3,2},{4,5},{5,4},{6,7},{7,6},{8,9},{9,8},{10,11... | collective-permute-start | bytes 49160 | tf_op jit(solution)/shard_map/ppermute | solution.py:135
  103.6 3.9 %collective-permute-start.1 = (f32[64,64]{1,0:T(8,128)S(1)}, f32[64,64]{1,0:T(8,128)S(1)}, u32[]{:S(2)}, u32[]{:S(2)}) collective-permute-start(f32[64,64]{1,0:T(8,128)S(1)} %add.21), channel_id=1, source_target_pairs={{0,2},{1,3},{2,0},{3,1},{4,6},{5,7},{6,4},{7,5},{8,10},{9,11},{10,... | collective-permute-start | bytes 49160 | tf_op jit(solution)/shard_map/ppermute | solution.py:135
  107.5 5.4 %collective-permute-start.2 = (f32[64,64]{1,0:T(8,128)S(1)}, f32[64,64]{1,0:T(8,128)S(1)}, u32[]{:S(2)}, u32[]{:S(2)}) collective-permute-start(f32[64,64]{1,0:T(8,128)S(1)} %add.22), channel_id=1, source_target_pairs={{0,4},{1,5},{2,6},{3,7},{4,0},{5,1},{6,2},{7,3},{8,12},{9,13},{10,... | collective-permute-start | bytes 49160 | tf_op jit(solution)/shard_map/ppermute | solution.py:135
  112.9 3.9 %collective-permute-start.3 = (f32[64,64]{1,0:T(8,128)S(1)}, f32[64,64]{1,0:T(8,128)S(1)}, u32[]{:S(2)}, u32[]{:S(2)}) collective-permute-start(f32[64,64]{1,0:T(8,128)S(1)} %add.23), channel_id=1, source_target_pairs={{0,8},{1,9},{2,10},{3,11},{4,12},{5,13},{6,14},{7,15},{8,0},{9,1},... | collective-permute-start | bytes 49160 | tf_op jit(solution)/shard_map/ppermute | solution.py:135
  116.8 5.4 %collective-permute-start.4 = (f32[64,64]{1,0:T(8,128)S(1)}, f32[64,64]{1,0:T(8,128)S(1)}, u32[]{:S(2)}, u32[]{:S(2)}) collective-permute-start(f32[64,64]{1,0:T(8,128)S(1)} %add.24), channel_id=1, source_target_pairs={{0,16},{1,17},{2,18},{3,19},{4,20},{5,21},{6,22},{7,23},{8,24},{9,... | collective-permute-start | bytes 49160 | tf_op jit(solution)/shard_map/ppermute | solution.py:135
  122.2 3.9 %collective-permute-start.5 = (f32[64,64]{1,0:T(8,128)S(1)}, f32[64,64]{1,0:T(8,128)S(1)}, u32[]{:S(2)}, u32[]{:S(2)}) collective-permute-start(f32[64,64]{1,0:T(8,128)S(1)} %add.25), channel_id=1, source_target_pairs={{0,32},{1,33},{2,34},{3,35},{4,36},{5,37},{6,38},{7,39},{8,40},{9,... | collective-permute-start | bytes 49160 | tf_op jit(solution)/shard_map/ppermute | solution.py:135
  126.2 5.4 %collective-permute-start.6 = (f32[64,64]{1,0:T(8,128)S(1)}, f32[64,64]{1,0:T(8,128)S(1)}, u32[]{:S(2)}, u32[]{:S(2)}) collective-permute-start(f32[64,64]{1,0:T(8,128)S(1)} %add.26), channel_id=1, source_target_pairs={{0,64},{1,65},{2,66},{3,67},{4,68},{5,69},{6,70},{7,71},{8,72},{9,... | collective-permute-start | bytes 49160 | tf_op jit(solution)/shard_map/ppermute | solution.py:135

commit v3 on v2

--- a/solution.py
+++ b/solution.py
@@ -14,9 +14,11 @@
 SEND_STEPS = 4
 
 
-def gather_outgoing(pod_basis, picks):
+def gather_outgoing(pod_basis, picks_by_ghost):
     rows_local, block_area = pod_basis.shape
-    count = picks.shape[0]
+    ghosts, dests = picks_by_ghost.shape
+    count = ghosts * dests
+    picks = picks_by_ghost.reshape(-1)
     sub = block_area // 128
 
     per_step = count // SEND_STEPS
@@ -29,7 +31,8 @@
             slab_ref[...] = pod_ref[...].reshape(rows_local, sub, 128)
 
         def one(n, carry):
-            out_ref[n] = slab_ref[pick_ref[step * per_step + n]]
+            n_all = step * per_step + n
+            out_ref[n] = slab_ref[pick_ref[(n_all % ghosts) * dests + n_all // ghosts]]
             return carry
 
         lax.fori_loop(0, per_step, one, 0, unroll=8)
@@ -53,7 +56,7 @@
     slots, rows, block_area = jac_by_slot.shape
     entries = table.shape[0]
     tile = ROW_TILE
-    flat_slots = column_slot.reshape(-1)
+    flat_slots = column_slot.T.reshape(-1)
 
     def body(col_ref, jac_ref, tab_ref, out_ref, part_ref, blocks_ref):
         step = pl.program_id(0)
@@ -75,7 +78,7 @@
             lhs = jac_ref[j].reshape(tile, BLOCK, BLOCK)
             picked = []
             for r in range(tile):
-                e = col_ref[(step * tile + r) * slots + j]
+                e = col_ref[j * rows + step * tile + r]
                 picked.append(blocks_ref[jnp.where(e >= 0, e, entries)])
             rhs = jnp.stack(picked)
             if j == 0:
@@ -123,16 +126,20 @@
     device_count = dom_count * outer_count
     ghost_lists = ghost_rows[:, 0, :]
     ghost_count = ghost_lists.shape[1]
-    outgoing = gather_outgoing(pod_basis, ghost_lists.reshape(-1))
+    outgoing = gather_outgoing(pod_basis, ghost_lists.T)
     outgoing = outgoing.reshape((device_count, ghost_count) + outgoing.shape[1:])
     received = lax.all_to_all(outgoing, ("dom", "outer"), split_axis=0, concat_axis=0, tiled=True)
     table = received.reshape((device_count * ghost_count,) + received.shape[2:])
     jac_by_slot = jnp.transpose(jacobian, (1, 0, 2))
     galerkin_rows, partial_value = block_products(jac_by_slot, table, column_slot)
     total = partial_value
-    for bit in range(device_count.bit_length() - 1):
-        pairs = [(i, i ^ (1 << bit)) for i in range(device_count)]
-        total = total + lax.ppermute(total, ("dom", "outer"), pairs)
+    for stride, span in ((1, 2), (2, 4), (8, 4), (32, 4)):
+        for flip in ((lambda d: 1 - d),) if span == 2 else ((lambda d: d ^ 1), (lambda d: 3 - d)):
+            pairs = []
+            for i in range(device_count):
+                digit = (i // stride) % span
+                pairs.append((i, i + (flip(digit) - digit) * stride))
+            total = total + lax.ppermute(total, ("dom", "outer"), pairs)
     reduced = total / math.sqrt(rows_local * device_count * BLOCK)
     return (galerkin_rows, reduced)
 

time: 133 us -> 132 us (level)
  blocking collectives: 0 us -> 64.3 us
  waiting for transfers between devices: 76.3 us -> 24.9 us
  starting transfers between devices: 16.4 us -> 3.64 us
  local copies, waits for them, and re-layouts: 2.39 us -> 0 us
  Pallas kernels: 35 us -> 37.1 us
    all_to_all x0 -> x1, blocking collectives: none -> 64.3 us  [on_device(): lax.all_to_all(outgoing, ('dom', 'outer'), split_axis=0, concat_axis=0, t...]
    all_to_all x1 -> x0, waiting for transfers between devices: 51.6 us -> none  [on_device(): lax.all_to_all(outgoing, ('dom', 'outer'), split_axis=0, concat_axis=0, t...]
    all_to_all x1 -> x0, starting transfers between devices: 11.7 us -> none  [on_device(): lax.all_to_all(outgoing, ('dom', 'outer'), split_axis=0, concat_axis=0, t...]
    pallas_call x1, Pallas kernels: 5.31 us -> 7.43 us  [gather_outgoing(): pl.pallas_call(body, grid_spec=grid_spec, out_shape=jax.ShapeDtypeStruct(...]
  transfers between devices with their start and end apart: 8 -> 7, of which waited for: 8 -> 7; matrix products, arithmetic and copies ran while one was open for 1% -> 0% of each run, Pallas kernels for 0% -> 0%
where the time goes in v3:
time: 132 us
  blocking collectives  64.3 us (49%)
  Pallas kernels  37.1 us (28%)
  waiting for transfers between devices  24.9 us (19%)
  starting transfers between devices  3.64 us (3%)
  other arithmetic  1.41 us (1%)
    all_to_all x1, blocking collectives, on_device(): lax.all_to_all(outgoing, ('dom', 'outer'), split_axis=0, concat_axis=0, t...  64.3 us
    pallas_call x1, Pallas kernels, block_products(): pl.pallas_call(body, grid_spec=grid_spec, out_shape=(jax.ShapeDtypeStruct...  29.6 us
    ppermute x7, waiting for transfers between devices, on_device(): total = total + lax.ppermute(total, ('dom', 'outer'), pairs)  24.9 us
    pallas_call x1, Pallas kernels, gather_outgoing(): pl.pallas_call(body, grid_spec=grid_spec, out_shape=jax.ShapeDtypeStruct(...  7.43 us
    ppermute x7, starting transfers between devices, on_device(): total = total + lax.ppermute(total, ('dom', 'outer'), pairs)  3.64 us
  transfers between devices with their start and end apart: 7, of which 7 were waited for; matrix products, arithmetic and copies ran while one was open for 0% of the time, Pallas kernels for 0%

profile of v3, /device:TPU:0, one launch (start us, length us, event | category | flops | bytes accessed | tf_op | source)
XLA Modules:
  0.0 131.9 jit_solution(13703163408415033210)
XLA Ops:
  0.6 7.4 %shard_map.59 = bf16[512,32,128]{2,1,0:T(8,128)(2,1)} custom-call(s32[512]{0:T(512)} %bitcast.15, bf16[128,4096]{1,0:T(8,128)(2,1)} %pod_ref.1), custom_call_target="tpu_custom_call" | custom-call | tf_op jit(solution)/shard_map/pallas_call | solution.py:47
  8.1 64.3 %all_to_all.5 = bf16[128,4,32,128]{3,2,1,0:T(8,128)(2,1)} all-to-all(bf16[128,4,32,128]{3,2,1,0:T(8,128)(2,1)} %bitcast.12), channel_id=1, replica_groups=mesh['dom'=16,'outer'=8] {'dom','outer'}, dimensions={0} | all-to-all | bytes 8388608 | tf_op jit(solution)/shard_map/all_to_all | solution.py:131
  72.3 29.6 %shard_map.60 = (bf16[128,4096]{1,0:T(8,128)(2,1)}, f32[64,64]{1,0:T(8,128)}) custom-call(s32[896]{0:T(1024)} %bitcast.14, bf16[7,128,4096]{2,1,0:T(8,128)(2,1)} %bitcast.13, bf16[512,32,128]{2,1,0:T(8,128)(2,1)} %bitcast.11), custom_call_target="tpu_custom_call" | custom-call | tf_op jit(solution)/shard_map/pallas_call | solution.py:111
  102.0 0.0 collective-permute-start
  102.0 1.4 %collective-permute-done = f32[64,64]{1,0:T(8,128)S(1)} collective-permute-done((f32[64,64]{1,0:T(8,128)}, f32[64,64]{1,0:T(8,128)S(1)}, u32[]{:S(2)}, u32[]{:S(2)}) %collective-permute-start) | collective-permute-done | bytes 16416 | tf_op jit(solution)/shard_map/ppermute | solution.py:142
  103.4 0.8 add.21
  104.2 0.4 collective-permute-start.1
  104.6 3.5 %collective-permute-done.1 = f32[64,64]{1,0:T(8,128)S(1)} collective-permute-done((f32[64,64]{1,0:T(8,128)S(1)}, f32[64,64]{1,0:T(8,128)S(1)}, u32[]{:S(2)}, u32[]{:S(2)}) %collective-permute-start.1) | collective-permute-done | bytes 16416 | tf_op jit(solution)/shard_map/ppermute | solution.py:142
  108.1 0.4 collective-permute-start.2
  108.5 4.7 %collective-permute-done.2 = f32[64,64]{1,0:T(8,128)S(1)} collective-permute-done((f32[64,64]{1,0:T(8,128)S(1)}, f32[64,64]{1,0:T(8,128)S(1)}, u32[]{:S(2)}, u32[]{:S(2)}) %collective-permute-start.2) | collective-permute-done | bytes 16416 | tf_op jit(solution)/shard_map/ppermute | solution.py:142
  113.2 0.6 collective-permute-start.3
  113.8 3.4 %collective-permute-done.3 = f32[64,64]{1,0:T(8,128)S(1)} collective-permute-done((f32[64,64]{1,0:T(8,128)S(1)}, f32[64,64]{1,0:T(8,128)S(1)}, u32[]{:S(2)}, u32[]{:S(2)}) %collective-permute-start.3) | collective-permute-done | bytes 16416 | tf_op jit(solution)/shard_map/ppermute | solution.py:142
  117.1 0.5 collective-permute-start.4
  117.6 4.6 %collective-permute-done.4 = f32[64,64]{1,0:T(8,128)S(1)} collective-permute-done((f32[64,64]{1,0:T(8,128)S(1)}, f32[64,64]{1,0:T(8,128)S(1)}, u32[]{:S(2)}, u32[]{:S(2)}) %collective-permute-start.4) | collective-permute-done | bytes 16416 | tf_op jit(solution)/shard_map/ppermute | solution.py:142
  122.3 0.5 collective-permute-start.5
  122.8 3.4 %collective-permute-done.5 = f32[64,64]{1,0:T(8,128)S(1)} collective-permute-done((f32[64,64]{1,0:T(8,128)S(1)}, f32[64,64]{1,0:T(8,128)S(1)}, u32[]{:S(2)}, u32[]{:S(2)}) %collective-permute-start.5) | collective-permute-done | bytes 16416 | tf_op jit(solution)/shard_map/ppermute | solution.py:142
  126.2 1.3 collective-permute-start.6
  127.5 3.8 %collective-permute-done.6 = f32[64,64]{1,0:T(8,128)S(1)} collective-permute-done((f32[64,64]{1,0:T(8,128)S(1)}, f32[64,64]{1,0:T(8,128)S(1)}, u32[]{:S(2)}, u32[]{:S(2)}) %collective-permute-start.6) | collective-permute-done | bytes 16416 | tf_op jit(solution)/shard_map/ppermute | solution.py:142
  131.3 0.6 add_multiply_fusion
  (5 shorter events, 0.0 us)
Async XLA Ops:
  102.0 1.4 %collective-permute-start = (f32[64,64]{1,0:T(8,128)}, f32[64,64]{1,0:T(8,128)S(1)}, u32[]{:S(2)}, u32[]{:S(2)}) collective-permute-start(f32[64,64]{1,0:T(8,128)} %get-tuple-element.5), channel_id=1, source_target_pairs={{0,1},{1,0},{2,3},{3,2},{4,5},{5,4},{6,7},{7,6},{8,9},{9,8},{10,11... | collective-permute-start | bytes 49160 | tf_op jit(solution)/shard_map/ppermute | solution.py:142
  104.2 3.9 %collective-permute-start.1 = (f32[64,64]{1,0:T(8,128)S(1)}, f32[64,64]{1,0:T(8,128)S(1)}, u32[]{:S(2)}, u32[]{:S(2)}) collective-permute-start(f32[64,64]{1,0:T(8,128)S(1)} %add.21), channel_id=1, source_target_pairs={{0,2},{1,3},{2,0},{3,1},{4,6},{5,7},{6,4},{7,5},{8,10},{9,11},{10,... | collective-permute-start | bytes 49160 | tf_op jit(solution)/shard_map/ppermute | solution.py:142
  108.1 5.1 %collective-permute-start.2 = (f32[64,64]{1,0:T(8,128)S(1)}, f32[64,64]{1,0:T(8,128)S(1)}, u32[]{:S(2)}, u32[]{:S(2)}) collective-permute-start(f32[64,64]{1,0:T(8,128)S(1)} %add.22), channel_id=1, source_target_pairs={{0,6},{1,7},{2,4},{3,5},{4,2},{5,3},{6,0},{7,1},{8,14},{9,15},{10,... | collective-permute-start | bytes 49160 | tf_op jit(solution)/shard_map/ppermute | solution.py:142
  113.2 3.9 %collective-permute-start.3 = (f32[64,64]{1,0:T(8,128)S(1)}, f32[64,64]{1,0:T(8,128)S(1)}, u32[]{:S(2)}, u32[]{:S(2)}) collective-permute-start(f32[64,64]{1,0:T(8,128)S(1)} %add.23), channel_id=1, source_target_pairs={{0,8},{1,9},{2,10},{3,11},{4,12},{5,13},{6,14},{7,15},{8,0},{9,1},... | collective-permute-start | bytes 49160 | tf_op jit(solution)/shard_map/ppermute | solution.py:142
  117.1 5.1 %collective-permute-start.4 = (f32[64,64]{1,0:T(8,128)S(1)}, f32[64,64]{1,0:T(8,128)S(1)}, u32[]{:S(2)}, u32[]{:S(2)}) collective-permute-start(f32[64,64]{1,0:T(8,128)S(1)} %add.24), channel_id=1, source_target_pairs={{0,24},{1,25},{2,26},{3,27},{4,28},{5,29},{6,30},{7,31},{8,16},{9,... | collective-permute-start | bytes 49160 | tf_op jit(solution)/shard_map/ppermute | solution.py:142
  122.3 3.9 %collective-permute-start.5 = (f32[64,64]{1,0:T(8,128)S(1)}, f32[64,64]{1,0:T(8,128)S(1)}, u32[]{:S(2)}, u32[]{:S(2)}) collective-permute-start(f32[64,64]{1,0:T(8,128)S(1)} %add.25), channel_id=1, source_target_pairs={{0,32},{1,33},{2,34},{3,35},{4,36},{5,37},{6,38},{7,39},{8,40},{9,... | collective-permute-start | bytes 49160 | tf_op jit(solution)/shard_map/ppermute | solution.py:142
  126.2 5.1 %collective-permute-start.6 = (f32[64,64]{1,0:T(8,128)S(1)}, f32[64,64]{1,0:T(8,128)S(1)}, u32[]{:S(2)}, u32[]{:S(2)}) collective-permute-start(f32[64,64]{1,0:T(8,128)S(1)} %add.26), channel_id=1, source_target_pairs={{0,96},{1,97},{2,98},{3,99},{4,100},{5,101},{6,102},{7,103},{8,104... | collective-permute-start | bytes 49160 | tf_op jit(solution)/shard_map/ppermute | solution.py:142

commit v4 on v3

--- a/solution.py
+++ b/solution.py
@@ -10,7 +10,7 @@
 BLOCK = 64
 MODES = 64
 SLOTS = 7
-ROW_TILE = 32
+ROW_TILE = 64
 SEND_STEPS = 4
 
 
@@ -22,6 +22,7 @@
     sub = block_area // 128
 
     per_step = count // SEND_STEPS
+    dests_per_step = dests // SEND_STEPS
 
     def body(pick_ref, pod_ref, out_ref, slab_ref):
         step = pl.program_id(0)
@@ -30,12 +31,13 @@
         def _():
             slab_ref[...] = pod_ref[...].reshape(rows_local, sub, 128)
 
-        def one(n, carry):
-            n_all = step * per_step + n
-            out_ref[n] = slab_ref[pick_ref[(n_all % ghosts) * dests + n_all // ghosts]]
+        def one(dl, carry):
+            d = step * dests_per_step + dl
+            for g in range(ghosts):
+                out_ref[dl * ghosts + g] = slab_ref[pick_ref[g * dests + d]]
             return carry
 
-        lax.fori_loop(0, per_step, one, 0, unroll=8)
+        lax.fori_loop(0, dests_per_step, one, 0, unroll=4)
 
     grid_spec = pltpu.PrefetchScalarGridSpec(
         num_scalar_prefetch=1,

time: 132 us -> 130 us (0.985)
  Pallas kernels: 37.1 us -> 34.7 us
    pallas_call x1, Pallas kernels: 7.43 us -> 5.17 us  [gather_outgoing(): pl.pallas_call(body, grid_spec=grid_spec, out_shape=jax.ShapeDtypeStruct(...]
where the time goes in v4:
time: 130 us
  blocking collectives  64.3 us (49%)
  Pallas kernels  34.7 us (27%)
  waiting for transfers between devices  24.9 us (19%)
  starting transfers between devices  3.65 us (3%)
  other arithmetic  1.41 us (1%)
    all_to_all x1, blocking collectives, on_device(): lax.all_to_all(outgoing, ('dom', 'outer'), split_axis=0, concat_axis=0, t...  64.3 us
    pallas_call x1, Pallas kernels, block_products(): pl.pallas_call(body, grid_spec=grid_spec, out_shape=(jax.ShapeDtypeStruct...  29.5 us
    ppermute x7, waiting for transfers between devices, on_device(): total = total + lax.ppermute(total, ('dom', 'outer'), pairs)  24.9 us
    pallas_call x1, Pallas kernels, gather_outgoing(): pl.pallas_call(body, grid_spec=grid_spec, out_shape=jax.ShapeDtypeStruct(...  5.17 us
    ppermute x7, starting transfers between devices, on_device(): total = total + lax.ppermute(total, ('dom', 'outer'), pairs)  3.65 us
  transfers between devices with their start and end apart: 7, of which 7 were waited for; matrix products, arithmetic and copies ran while one was open for 0% of the time, Pallas kernels for 0%

profile of v4, /device:TPU:0, one launch (start us, length us, event | category | flops | bytes accessed | tf_op | source)
XLA Modules:
  0.0 129.6 jit_solution(11413040530327041840)
XLA Ops:
  0.6 5.2 %shard_map.59 = bf16[512,32,128]{2,1,0:T(8,128)(2,1)} custom-call(s32[512]{0:T(512)} %bitcast.15, bf16[128,4096]{1,0:T(8,128)(2,1)} %pod_ref.1), custom_call_target="tpu_custom_call" | custom-call | tf_op jit(solution)/shard_map/pallas_call | solution.py:49
  5.8 64.3 %all_to_all.5 = bf16[128,4,32,128]{3,2,1,0:T(8,128)(2,1)} all-to-all(bf16[128,4,32,128]{3,2,1,0:T(8,128)(2,1)} %bitcast.12), channel_id=1, replica_groups=mesh['dom'=16,'outer'=8] {'dom','outer'}, dimensions={0} | all-to-all | bytes 8388608 | tf_op jit(solution)/shard_map/all_to_all | solution.py:133
  70.1 29.5 %shard_map.60 = (bf16[128,4096]{1,0:T(8,128)(2,1)}, f32[64,64]{1,0:T(8,128)}) custom-call(s32[896]{0:T(1024)} %bitcast.14, bf16[7,128,4096]{2,1,0:T(8,128)(2,1)} %bitcast.13, bf16[512,32,128]{2,1,0:T(8,128)(2,1)} %bitcast.11), custom_call_target="tpu_custom_call" | custom-call | tf_op jit(solution)/shard_map/pallas_call | solution.py:113
  99.6 0.0 collective-permute-start
  99.6 1.4 %collective-permute-done = f32[64,64]{1,0:T(8,128)S(1)} collective-permute-done((f32[64,64]{1,0:T(8,128)}, f32[64,64]{1,0:T(8,128)S(1)}, u32[]{:S(2)}, u32[]{:S(2)}) %collective-permute-start) | collective-permute-done | bytes 16416 | tf_op jit(solution)/shard_map/ppermute | solution.py:144
  101.0 0.8 add.21
  101.8 0.4 collective-permute-start.1
  102.2 3.5 %collective-permute-done.1 = f32[64,64]{1,0:T(8,128)S(1)} collective-permute-done((f32[64,64]{1,0:T(8,128)S(1)}, f32[64,64]{1,0:T(8,128)S(1)}, u32[]{:S(2)}, u32[]{:S(2)}) %collective-permute-start.1) | collective-permute-done | bytes 16416 | tf_op jit(solution)/shard_map/ppermute | solution.py:144
  105.7 0.4 collective-permute-start.2
  106.1 4.7 %collective-permute-done.2 = f32[64,64]{1,0:T(8,128)S(1)} collective-permute-done((f32[64,64]{1,0:T(8,128)S(1)}, f32[64,64]{1,0:T(8,128)S(1)}, u32[]{:S(2)}, u32[]{:S(2)}) %collective-permute-start.2) | collective-permute-done | bytes 16416 | tf_op jit(solution)/shard_map/ppermute | solution.py:144
  110.8 0.6 collective-permute-start.3
  111.4 3.4 %collective-permute-done.3 = f32[64,64]{1,0:T(8,128)S(1)} collective-permute-done((f32[64,64]{1,0:T(8,128)S(1)}, f32[64,64]{1,0:T(8,128)S(1)}, u32[]{:S(2)}, u32[]{:S(2)}) %collective-permute-start.3) | collective-permute-done | bytes 16416 | tf_op jit(solution)/shard_map/ppermute | solution.py:144
  114.8 0.5 collective-permute-start.4
  115.3 4.6 %collective-permute-done.4 = f32[64,64]{1,0:T(8,128)S(1)} collective-permute-done((f32[64,64]{1,0:T(8,128)S(1)}, f32[64,64]{1,0:T(8,128)S(1)}, u32[]{:S(2)}, u32[]{:S(2)}) %collective-permute-start.4) | collective-permute-done | bytes 16416 | tf_op jit(solution)/shard_map/ppermute | solution.py:144
  119.9 0.5 collective-permute-start.5
  120.4 3.4 %collective-permute-done.5 = f32[64,64]{1,0:T(8,128)S(1)} collective-permute-done((f32[64,64]{1,0:T(8,128)S(1)}, f32[64,64]{1,0:T(8,128)S(1)}, u32[]{:S(2)}, u32[]{:S(2)}) %collective-permute-start.5) | collective-permute-done | bytes 16416 | tf_op jit(solution)/shard_map/ppermute | solution.py:144
  123.8 1.3 %collective-permute-start.6 = (f32[64,64]{1,0:T(8,128)S(1)}, f32[64,64]{1,0:T(8,128)S(1)}, u32[]{:S(2)}, u32[]{:S(2)}) collective-permute-start(f32[64,64]{1,0:T(8,128)S(1)} %add.26), channel_id=1, source_target_pairs={{0,96},{1,97},{2,98},{3,99},{4,100},{5,101},{6,102},{7,103},{8,104... | collective-permute-start | bytes 49160 | tf_op jit(solution)/shard_map/ppermute | solution.py:144
  125.1 3.8 %collective-permute-done.6 = f32[64,64]{1,0:T(8,128)S(1)} collective-permute-done((f32[64,64]{1,0:T(8,128)S(1)}, f32[64,64]{1,0:T(8,128)S(1)}, u32[]{:S(2)}, u32[]{:S(2)}) %collective-permute-start.6) | collective-permute-done | bytes 16416 | tf_op jit(solution)/shard_map/ppermute | solution.py:144
  128.9 0.6 add_multiply_fusion
  (5 shorter events, 0.0 us)
Async XLA Ops:
  99.6 1.4 %collective-permute-start = (f32[64,64]{1,0:T(8,128)}, f32[64,64]{1,0:T(8,128)S(1)}, u32[]{:S(2)}, u32[]{:S(2)}) collective-permute-start(f32[64,64]{1,0:T(8,128)} %get-tuple-element.5), channel_id=1, source_target_pairs={{0,1},{1,0},{2,3},{3,2},{4,5},{5,4},{6,7},{7,6},{8,9},{9,8},{10,11... | collective-permute-start | bytes 49160 | tf_op jit(solution)/shard_map/ppermute | solution.py:144
  101.8 3.9 %collective-permute-start.1 = (f32[64,64]{1,0:T(8,128)S(1)}, f32[64,64]{1,0:T(8,128)S(1)}, u32[]{:S(2)}, u32[]{:S(2)}) collective-permute-start(f32[64,64]{1,0:T(8,128)S(1)} %add.21), channel_id=1, source_target_pairs={{0,2},{1,3},{2,0},{3,1},{4,6},{5,7},{6,4},{7,5},{8,10},{9,11},{10,... | collective-permute-start | bytes 49160 | tf_op jit(solution)/shard_map/ppermute | solution.py:144
  105.7 5.1 %collective-permute-start.2 = (f32[64,64]{1,0:T(8,128)S(1)}, f32[64,64]{1,0:T(8,128)S(1)}, u32[]{:S(2)}, u32[]{:S(2)}) collective-permute-start(f32[64,64]{1,0:T(8,128)S(1)} %add.22), channel_id=1, source_target_pairs={{0,6},{1,7},{2,4},{3,5},{4,2},{5,3},{6,0},{7,1},{8,14},{9,15},{10,... | collective-permute-start | bytes 49160 | tf_op jit(solution)/shard_map/ppermute | solution.py:144
  110.8 3.9 %collective-permute-start.3 = (f32[64,64]{1,0:T(8,128)S(1)}, f32[64,64]{1,0:T(8,128)S(1)}, u32[]{:S(2)}, u32[]{:S(2)}) collective-permute-start(f32[64,64]{1,0:T(8,128)S(1)} %add.23), channel_id=1, source_target_pairs={{0,8},{1,9},{2,10},{3,11},{4,12},{5,13},{6,14},{7,15},{8,0},{9,1},... | collective-permute-start | bytes 49160 | tf_op jit(solution)/shard_map/ppermute | solution.py:144
  114.8 5.1 %collective-permute-start.4 = (f32[64,64]{1,0:T(8,128)S(1)}, f32[64,64]{1,0:T(8,128)S(1)}, u32[]{:S(2)}, u32[]{:S(2)}) collective-permute-start(f32[64,64]{1,0:T(8,128)S(1)} %add.24), channel_id=1, source_target_pairs={{0,24},{1,25},{2,26},{3,27},{4,28},{5,29},{6,30},{7,31},{8,16},{9,... | collective-permute-start | bytes 49160 | tf_op jit(solution)/shard_map/ppermute | solution.py:144
  119.9 3.9 %collective-permute-start.5 = (f32[64,64]{1,0:T(8,128)S(1)}, f32[64,64]{1,0:T(8,128)S(1)}, u32[]{:S(2)}, u32[]{:S(2)}) collective-permute-start(f32[64,64]{1,0:T(8,128)S(1)} %add.25), channel_id=1, source_target_pairs={{0,32},{1,33},{2,34},{3,35},{4,36},{5,37},{6,38},{7,39},{8,40},{9,... | collective-permute-start | bytes 49160 | tf_op jit(solution)/shard_map/ppermute | solution.py:144
  123.8 5.1 %collective-permute-start.6 = (f32[64,64]{1,0:T(8,128)S(1)}, f32[64,64]{1,0:T(8,128)S(1)}, u32[]{:S(2)}, u32[]{:S(2)}) collective-permute-start(f32[64,64]{1,0:T(8,128)S(1)} %add.26), channel_id=1, source_target_pairs={{0,96},{1,97},{2,98},{3,99},{4,100},{5,101},{6,102},{7,103},{8,104... | collective-permute-start | bytes 49160 | tf_op jit(solution)/shard_map/ppermute | solution.py:144

commit v5 on v4

--- a/solution.py
+++ b/solution.py
@@ -54,8 +54,26 @@
     )(picks, pod_basis)
 
 
+def relayout_jacobian(jac_by_slot):
+    slots, rows, block_area = jac_by_slot.shape
+    tile = ROW_TILE
+
+    def body(jac_ref, out_ref):
+        for j in range(slots):
+            out_ref[j] = jac_ref[j].reshape(tile, BLOCK, BLOCK)
+
+    return pl.pallas_call(
+        body,
+        grid=(rows // tile,),
+        in_specs=[pl.BlockSpec((slots, tile, block_area), lambda i: (0, i, 0))],
+        out_specs=pl.BlockSpec((slots, tile, BLOCK, BLOCK), lambda i: (0, i, 0, 0)),
+        out_shape=jax.ShapeDtypeStruct((slots, rows, BLOCK, BLOCK), jac_by_slot.dtype),
+    )(jac_by_slot)
+
+
 def block_products(jac_by_slot, table, column_slot):
-    slots, rows, block_area = jac_by_slot.shape
+    slots, rows = jac_by_slot.shape[:2]
+    block_area = BLOCK * MODES
     entries = table.shape[0]
     tile = ROW_TILE
     flat_slots = column_slot.T.reshape(-1)
@@ -77,7 +95,7 @@
         acc = jnp.zeros((tile, BLOCK, MODES), jnp.float32)
         diag = None
         for j in range(slots):
-            lhs = jac_ref[j].reshape(tile, BLOCK, BLOCK)
+            lhs = jac_ref[j]
             picked = []
             for r in range(tile):
                 e = col_ref[j * rows + step * tile + r]
@@ -101,7 +119,7 @@
         num_scalar_prefetch=1,
         grid=(rows // tile,),
         in_specs=[
-            pl.BlockSpec((slots, tile, block_area), lambda i, c: (0, i, 0)),
+            pl.BlockSpec((slots, tile, BLOCK, BLOCK), lambda i, c: (0, i, 0, 0)),
             pl.BlockSpec(table.shape, lambda i, c: (0, 0, 0)),
         ],
         out_specs=[
@@ -132,7 +150,7 @@
     outgoing = outgoing.reshape((device_count, ghost_count) + outgoing.shape[1:])
     received = lax.all_to_all(outgoing, ("dom", "outer"), split_axis=0, concat_axis=0, tiled=True)
     table = received.reshape((device_count * ghost_count,) + received.shape[2:])
-    jac_by_slot = jnp.transpose(jacobian, (1, 0, 2))
+    jac_by_slot = relayout_jacobian(jnp.transpose(jacobian, (1, 0, 2)))
     galerkin_rows, partial_value = block_products(jac_by_slot, table, column_slot)
     total = partial_value
     for stride, span in ((1, 2), (2, 4), (8, 4), (32, 4)):

time: 130 us -> 129 us (level)
  blocking collectives: 64.3 us -> 0 us
  waiting for transfers between devices: 24.9 us -> 66.2 us
  starting transfers between devices: 3.65 us -> 15.4 us
  Pallas kernels: 34.7 us -> 44.8 us
    all_to_all x1 -> x0, blocking collectives: 64.3 us -> none  [on_device(): lax.all_to_all(outgoing, ('dom', 'outer'), split_axis=0, concat_axis=0, t...]
    all_to_all x0 -> x1, waiting for transfers between devices: none -> 41.4 us  [on_device(): lax.all_to_all(outgoing, ('dom', 'outer'), split_axis=0, concat_axis=0, t...]
    all_to_all x0 -> x1, starting transfers between devices: none -> 11.7 us  [on_device(): lax.all_to_all(outgoing, ('dom', 'outer'), split_axis=0, concat_axis=0, t...]
    pallas_call x0 -> x1, Pallas kernels: none -> 11.2 us  [relayout_jacobian(): pl.pallas_call(body, grid=(rows // tile,), in_specs=[pl.BlockSpec((slots,...]
  transfers between devices with their start and end apart: 7 -> 8, of which waited for: 7 -> 8; matrix products, arithmetic and copies ran while one was open for 0% -> 0% of each run, Pallas kernels for 0% -> 9%
where the time goes in v5:
time: 129 us
  waiting for transfers between devices  66.2 us (51%)
  Pallas kernels  44.8 us (35%)
  starting transfers between devices  15.4 us (12%)
  other arithmetic  1.41 us (1%)
    all_to_all x1, waiting for transfers between devices, on_device(): lax.all_to_all(outgoing, ('dom', 'outer'), split_axis=0, concat_axis=0, t...  41.4 us
    pallas_call x1, Pallas kernels, block_products(): pl.pallas_call(body, grid_spec=grid_spec, out_shape=(jax.ShapeDtypeStruct...  28.5 us
    ppermute x7, waiting for transfers between devices, on_device(): total = total + lax.ppermute(total, ('dom', 'outer'), pairs)  24.9 us
    all_to_all x1, starting transfers between devices, on_device(): lax.all_to_all(outgoing, ('dom', 'outer'), split_axis=0, concat_axis=0, t...  11.7 us
    pallas_call x1, Pallas kernels, relayout_jacobian(): pl.pallas_call(body, grid=(rows // tile,), in_specs=[pl.BlockSpec((slots,...  11.2 us
    pallas_call x1, Pallas kernels, gather_outgoing(): pl.pallas_call(body, grid_spec=grid_spec, out_shape=jax.ShapeDtypeStruct(...  5.14 us
    ppermute x7, starting transfers between devices, on_device(): total = total + lax.ppermute(total, ('dom', 'outer'), pairs)  3.67 us
  transfers between devices with their start and end apart: 8, of which 8 were waited for; matrix products, arithmetic and copies ran while one was open for 0% of the time, Pallas kernels for 9%

profile of v5, /device:TPU:0, one launch (start us, length us, event | category | flops | bytes accessed | tf_op | source)
XLA Modules:
  0.0 128.5 jit_solution(18036773887595381257)
XLA Ops:
  0.6 5.1 %shard_map.60 = bf16[512,32,128]{2,1,0:T(8,128)(2,1)} custom-call(s32[512]{0:T(512)} %bitcast.14, bf16[128,4096]{1,0:T(8,128)(2,1)} %pod_ref.1), custom_call_target="tpu_custom_call" | custom-call | tf_op jit(solution)/shard_map/pallas_call | solution.py:49
  5.8 11.7 %all-to-all-start = ((bf16[128,4,32,128]{3,2,1,0:T(8,128)(2,1)}), bf16[128,4,32,128]{3,2,1,0:T(8,128)(2,1)}, u32[]{:S(2)}, u32[]{:S(2)}) async-start(bf16[128,4,32,128]{3,2,1,0:T(8,128)(2,1)} %bitcast.11), calls=%async_computation | async-start | bytes 8388608 | tf_op jit(solution)/shard_map/all_to_all | solution.py:151
  17.5 11.2 %shard_map.59.jac_ref = bf16[7,128,64,64]{3,2,1,0:T(8,128)(2,1)} custom-call(bf16[7,128,4096]{2,1,0:T(8,128)(2,1)} %bitcast.12), custom_call_target="tpu_custom_call" | custom-call | tf_op jit(solution)/shard_map/pallas_call | solution.py:65
  28.7 41.4 %all-to-all-done = bf16[128,4,32,128]{3,2,1,0:T(8,128)(2,1)} async-done(((bf16[128,4,32,128]{3,2,1,0:T(8,128)(2,1)}), bf16[128,4,32,128]{3,2,1,0:T(8,128)(2,1)}, u32[]{:S(2)}, u32[]{:S(2)}) %all-to-all-start) | async-done | bytes 4194336 | tf_op jit(solution)/shard_map/all_to_all | solution.py:151
  70.1 28.5 %shard_map.61 = (bf16[128,4096]{1,0:T(8,128)(2,1)}, f32[64,64]{1,0:T(8,128)}) custom-call(s32[896]{0:T(1024)} %bitcast.13, bf16[7,128,64,64]{3,2,1,0:T(8,128)(2,1)} %shard_map.59.jac_ref, bf16[512,32,128]{2,1,0:T(8,128)(2,1)} %bitcast.7.tab_ref), custom_call_target="tpu_custom_call" | custom-call | tf_op jit(solution)/shard_map/pallas_call | solution.py:131
  98.6 0.0 collective-permute-start
  98.6 1.4 %collective-permute-done = f32[64,64]{1,0:T(8,128)S(1)} collective-permute-done((f32[64,64]{1,0:T(8,128)}, f32[64,64]{1,0:T(8,128)S(1)}, u32[]{:S(2)}, u32[]{:S(2)}) %collective-permute-start) | collective-permute-done | bytes 16416 | tf_op jit(solution)/shard_map/ppermute | solution.py:162
  100.0 0.8 add.21
  100.8 0.4 collective-permute-start.1
  101.2 3.5 %collective-permute-done.1 = f32[64,64]{1,0:T(8,128)S(1)} collective-permute-done((f32[64,64]{1,0:T(8,128)S(1)}, f32[64,64]{1,0:T(8,128)S(1)}, u32[]{:S(2)}, u32[]{:S(2)}) %collective-permute-start.1) | collective-permute-done | bytes 16416 | tf_op jit(solution)/shard_map/ppermute | solution.py:162
  104.7 0.4 collective-permute-start.2
  105.1 4.7 %collective-permute-done.2 = f32[64,64]{1,0:T(8,128)S(1)} collective-permute-done((f32[64,64]{1,0:T(8,128)S(1)}, f32[64,64]{1,0:T(8,128)S(1)}, u32[]{:S(2)}, u32[]{:S(2)}) %collective-permute-start.2) | collective-permute-done | bytes 16416 | tf_op jit(solution)/shard_map/ppermute | solution.py:162
  109.8 0.6 collective-permute-start.3
  110.4 3.4 %collective-permute-done.3 = f32[64,64]{1,0:T(8,128)S(1)} collective-permute-done((f32[64,64]{1,0:T(8,128)S(1)}, f32[64,64]{1,0:T(8,128)S(1)}, u32[]{:S(2)}, u32[]{:S(2)}) %collective-permute-start.3) | collective-permute-done | bytes 16416 | tf_op jit(solution)/shard_map/ppermute | solution.py:162
  113.7 0.5 collective-permute-start.4
  114.2 4.6 %collective-permute-done.4 = f32[64,64]{1,0:T(8,128)S(1)} collective-permute-done((f32[64,64]{1,0:T(8,128)S(1)}, f32[64,64]{1,0:T(8,128)S(1)}, u32[]{:S(2)}, u32[]{:S(2)}) %collective-permute-start.4) | collective-permute-done | bytes 16416 | tf_op jit(solution)/shard_map/ppermute | solution.py:162
  118.9 0.5 collective-permute-start.5
  119.4 3.4 %collective-permute-done.5 = f32[64,64]{1,0:T(8,128)S(1)} collective-permute-done((f32[64,64]{1,0:T(8,128)S(1)}, f32[64,64]{1,0:T(8,128)S(1)}, u32[]{:S(2)}, u32[]{:S(2)}) %collective-permute-start.5) | collective-permute-done | bytes 16416 | tf_op jit(solution)/shard_map/ppermute | solution.py:162
  122.8 1.3 %collective-permute-start.6 = (f32[64,64]{1,0:T(8,128)S(1)}, f32[64,64]{1,0:T(8,128)S(1)}, u32[]{:S(2)}, u32[]{:S(2)}) collective-permute-start(f32[64,64]{1,0:T(8,128)S(1)} %add.26), channel_id=1, source_target_pairs={{0,96},{1,97},{2,98},{3,99},{4,100},{5,101},{6,102},{7,103},{8,104... | collective-permute-start | bytes 49160 | tf_op jit(solution)/shard_map/ppermute | solution.py:162
  124.1 3.8 %collective-permute-done.6 = f32[64,64]{1,0:T(8,128)S(1)} collective-permute-done((f32[64,64]{1,0:T(8,128)S(1)}, f32[64,64]{1,0:T(8,128)S(1)}, u32[]{:S(2)}, u32[]{:S(2)}) %collective-permute-start.6) | collective-permute-done | bytes 16416 | tf_op jit(solution)/shard_map/ppermute | solution.py:162
  127.9 0.6 add_multiply_fusion
  (5 shorter events, 0.0 us)
Async XLA Ops:
  5.8 64.3 %all-to-all-start = ((bf16[128,4,32,128]{3,2,1,0:T(8,128)(2,1)}), bf16[128,4,32,128]{3,2,1,0:T(8,128)(2,1)}, u32[]{:S(2)}, u32[]{:S(2)}) async-start(bf16[128,4,32,128]{3,2,1,0:T(8,128)(2,1)} %bitcast.11), calls=%async_computation | async-start | bytes 8388608 | tf_op jit(solution)/shard_map/all_to_all | solution.py:151
  98.6 1.4 %collective-permute-start = (f32[64,64]{1,0:T(8,128)}, f32[64,64]{1,0:T(8,128)S(1)}, u32[]{:S(2)}, u32[]{:S(2)}) collective-permute-start(f32[64,64]{1,0:T(8,128)} %get-tuple-element.5), channel_id=1, source_target_pairs={{0,1},{1,0},{2,3},{3,2},{4,5},{5,4},{6,7},{7,6},{8,9},{9,8},{10,11... | collective-permute-start | bytes 49160 | tf_op jit(solution)/shard_map/ppermute | solution.py:162
  100.8 3.9 %collective-permute-start.1 = (f32[64,64]{1,0:T(8,128)S(1)}, f32[64,64]{1,0:T(8,128)S(1)}, u32[]{:S(2)}, u32[]{:S(2)}) collective-permute-start(f32[64,64]{1,0:T(8,128)S(1)} %add.21), channel_id=1, source_target_pairs={{0,2},{1,3},{2,0},{3,1},{4,6},{5,7},{6,4},{7,5},{8,10},{9,11},{10,... | collective-permute-start | bytes 49160 | tf_op jit(solution)/shard_map/ppermute | solution.py:162
  104.7 5.1 %collective-permute-start.2 = (f32[64,64]{1,0:T(8,128)S(1)}, f32[64,64]{1,0:T(8,128)S(1)}, u32[]{:S(2)}, u32[]{:S(2)}) collective-permute-start(f32[64,64]{1,0:T(8,128)S(1)} %add.22), channel_id=1, source_target_pairs={{0,6},{1,7},{2,4},{3,5},{4,2},{5,3},{6,0},{7,1},{8,14},{9,15},{10,... | collective-permute-start | bytes 49160 | tf_op jit(solution)/shard_map/ppermute | solution.py:162
  109.8 3.9 %collective-permute-start.3 = (f32[64,64]{1,0:T(8,128)S(1)}, f32[64,64]{1,0:T(8,128)S(1)}, u32[]{:S(2)}, u32[]{:S(2)}) collective-permute-start(f32[64,64]{1,0:T(8,128)S(1)} %add.23), channel_id=1, source_target_pairs={{0,8},{1,9},{2,10},{3,11},{4,12},{5,13},{6,14},{7,15},{8,0},{9,1},... | collective-permute-start | bytes 49160 | tf_op jit(solution)/shard_map/ppermute | solution.py:162
  113.7 5.1 %collective-permute-start.4 = (f32[64,64]{1,0:T(8,128)S(1)}, f32[64,64]{1,0:T(8,128)S(1)}, u32[]{:S(2)}, u32[]{:S(2)}) collective-permute-start(f32[64,64]{1,0:T(8,128)S(1)} %add.24), channel_id=1, source_target_pairs={{0,24},{1,25},{2,26},{3,27},{4,28},{5,29},{6,30},{7,31},{8,16},{9,... | collective-permute-start | bytes 49160 | tf_op jit(solution)/shard_map/ppermute | solution.py:162
  118.9 3.9 %collective-permute-start.5 = (f32[64,64]{1,0:T(8,128)S(1)}, f32[64,64]{1,0:T(8,128)S(1)}, u32[]{:S(2)}, u32[]{:S(2)}) collective-permute-start(f32[64,64]{1,0:T(8,128)S(1)} %add.25), channel_id=1, source_target_pairs={{0,32},{1,33},{2,34},{3,35},{4,36},{5,37},{6,38},{7,39},{8,40},{9,... | collective-permute-start | bytes 49160 | tf_op jit(solution)/shard_map/ppermute | solution.py:162
  122.8 5.1 %collective-permute-start.6 = (f32[64,64]{1,0:T(8,128)S(1)}, f32[64,64]{1,0:T(8,128)S(1)}, u32[]{:S(2)}, u32[]{:S(2)}) collective-permute-start(f32[64,64]{1,0:T(8,128)S(1)} %add.26), channel_id=1, source_target_pairs={{0,96},{1,97},{2,98},{3,99},{4,100},{5,101},{6,102},{7,103},{8,104... | collective-permute-start | bytes 49160 | tf_op jit(solution)/shard_map/ppermute | solution.py:162

commit v6 on v5

--- a/solution.py
+++ b/solution.py
@@ -10,7 +10,8 @@
 BLOCK = 64
 MODES = 64
 SLOTS = 7
-ROW_TILE = 64
+ROW_TILE = 32
+RELAYOUT_TILE = 64
 SEND_STEPS = 4
 
 
@@ -56,7 +57,7 @@
 
 def relayout_jacobian(jac_by_slot):
     slots, rows, block_area = jac_by_slot.shape
-    tile = ROW_TILE
+    tile = RELAYOUT_TILE
 
     def body(jac_ref, out_ref):
         for j in range(slots):

time: 129 us -> 130 us (level)
  no operation moved by 1% of the time
where the time goes in v6:
time: 130 us; the launch traced here: 129 us
  waiting for transfers between devices  66.3 us (51%)
  Pallas kernels  45.7 us (35%)
  starting transfers between devices  15.4 us (12%)
  other arithmetic  1.41 us (1%)
    all_to_all x1, waiting for transfers between devices, on_device(): lax.all_to_all(outgoing, ('dom', 'outer'), split_axis=0, concat_axis=0, t...  41.4 us
    pallas_call x1, Pallas kernels, block_products(): pl.pallas_call(body, grid_spec=grid_spec, out_shape=(jax.ShapeDtypeStruct...  29.3 us
    ppermute x7, waiting for transfers between devices, on_device(): total = total + lax.ppermute(total, ('dom', 'outer'), pairs)  24.9 us
    all_to_all x1, starting transfers between devices, on_device(): lax.all_to_all(outgoing, ('dom', 'outer'), split_axis=0, concat_axis=0, t...  11.7 us
    pallas_call x1, Pallas kernels, relayout_jacobian(): pl.pallas_call(body, grid=(rows // tile,), in_specs=[pl.BlockSpec((slots,...  11.2 us
    pallas_call x1, Pallas kernels, gather_outgoing(): pl.pallas_call(body, grid_spec=grid_spec, out_shape=jax.ShapeDtypeStruct(...  5.14 us
    ppermute x7, starting transfers between devices, on_device(): total = total + lax.ppermute(total, ('dom', 'outer'), pairs)  3.66 us
  transfers between devices with their start and end apart: 8, of which 8 were waited for; matrix products, arithmetic and copies ran while one was open for 0% of the time, Pallas kernels for 9%

profile of v6, /device:TPU:0, one launch (start us, length us, event | category | flops | bytes accessed | tf_op | source)
XLA Modules:
  0.0 129.4 jit_solution(14435850742392823759)
XLA Ops:
  0.6 5.1 %shard_map.60 = bf16[512,32,128]{2,1,0:T(8,128)(2,1)} custom-call(s32[512]{0:T(512)} %bitcast.14, bf16[128,4096]{1,0:T(8,128)(2,1)} %pod_ref.1), custom_call_target="tpu_custom_call" | custom-call | tf_op jit(solution)/shard_map/pallas_call | solution.py:50
  5.8 11.7 %all-to-all-start = ((bf16[128,4,32,128]{3,2,1,0:T(8,128)(2,1)}), bf16[128,4,32,128]{3,2,1,0:T(8,128)(2,1)}, u32[]{:S(2)}, u32[]{:S(2)}) async-start(bf16[128,4,32,128]{3,2,1,0:T(8,128)(2,1)} %bitcast.11), calls=%async_computation | async-start | bytes 8388608 | tf_op jit(solution)/shard_map/all_to_all | solution.py:152
  17.5 11.2 %shard_map.59.jac_ref = bf16[7,128,64,64]{3,2,1,0:T(8,128)(2,1)} custom-call(bf16[7,128,4096]{2,1,0:T(8,128)(2,1)} %bitcast.12), custom_call_target="tpu_custom_call" | custom-call | tf_op jit(solution)/shard_map/pallas_call | solution.py:66
  28.7 41.4 %all-to-all-done = bf16[128,4,32,128]{3,2,1,0:T(8,128)(2,1)} async-done(((bf16[128,4,32,128]{3,2,1,0:T(8,128)(2,1)}), bf16[128,4,32,128]{3,2,1,0:T(8,128)(2,1)}, u32[]{:S(2)}, u32[]{:S(2)}) %all-to-all-start) | async-done | bytes 4194336 | tf_op jit(solution)/shard_map/all_to_all | solution.py:152
  70.0 29.3 %shard_map.61 = (bf16[128,4096]{1,0:T(8,128)(2,1)}, f32[64,64]{1,0:T(8,128)}) custom-call(s32[896]{0:T(1024)} %bitcast.13, bf16[7,128,64,64]{3,2,1,0:T(8,128)(2,1)} %shard_map.59.jac_ref, bf16[512,32,128]{2,1,0:T(8,128)(2,1)} %bitcast.7.tab_ref), custom_call_target="tpu_custom_call" | custom-call | tf_op jit(solution)/shard_map/pallas_call | solution.py:132
  99.4 0.0 collective-permute-start
  99.4 1.4 %collective-permute-done = f32[64,64]{1,0:T(8,128)S(1)} collective-permute-done((f32[64,64]{1,0:T(8,128)}, f32[64,64]{1,0:T(8,128)S(1)}, u32[]{:S(2)}, u32[]{:S(2)}) %collective-permute-start) | collective-permute-done | bytes 16416 | tf_op jit(solution)/shard_map/ppermute | solution.py:163
  100.8 0.8 add.21
  101.6 0.4 collective-permute-start.1
  102.0 3.5 %collective-permute-done.1 = f32[64,64]{1,0:T(8,128)S(1)} collective-permute-done((f32[64,64]{1,0:T(8,128)S(1)}, f32[64,64]{1,0:T(8,128)S(1)}, u32[]{:S(2)}, u32[]{:S(2)}) %collective-permute-start.1) | collective-permute-done | bytes 16416 | tf_op jit(solution)/shard_map/ppermute | solution.py:163
  105.5 0.4 collective-permute-start.2
  105.9 4.7 %collective-permute-done.2 = f32[64,64]{1,0:T(8,128)S(1)} collective-permute-done((f32[64,64]{1,0:T(8,128)S(1)}, f32[64,64]{1,0:T(8,128)S(1)}, u32[]{:S(2)}, u32[]{:S(2)}) %collective-permute-start.2) | collective-permute-done | bytes 16416 | tf_op jit(solution)/shard_map/ppermute | solution.py:163
  110.6 0.6 collective-permute-start.3
  111.2 3.4 %collective-permute-done.3 = f32[64,64]{1,0:T(8,128)S(1)} collective-permute-done((f32[64,64]{1,0:T(8,128)S(1)}, f32[64,64]{1,0:T(8,128)S(1)}, u32[]{:S(2)}, u32[]{:S(2)}) %collective-permute-start.3) | collective-permute-done | bytes 16416 | tf_op jit(solution)/shard_map/ppermute | solution.py:163
  114.6 0.5 collective-permute-start.4
  115.0 4.6 %collective-permute-done.4 = f32[64,64]{1,0:T(8,128)S(1)} collective-permute-done((f32[64,64]{1,0:T(8,128)S(1)}, f32[64,64]{1,0:T(8,128)S(1)}, u32[]{:S(2)}, u32[]{:S(2)}) %collective-permute-start.4) | collective-permute-done | bytes 16416 | tf_op jit(solution)/shard_map/ppermute | solution.py:163
  119.7 0.5 collective-permute-start.5
  120.2 3.4 %collective-permute-done.5 = f32[64,64]{1,0:T(8,128)S(1)} collective-permute-done((f32[64,64]{1,0:T(8,128)S(1)}, f32[64,64]{1,0:T(8,128)S(1)}, u32[]{:S(2)}, u32[]{:S(2)}) %collective-permute-start.5) | collective-permute-done | bytes 16416 | tf_op jit(solution)/shard_map/ppermute | solution.py:163
  123.6 1.3 %collective-permute-start.6 = (f32[64,64]{1,0:T(8,128)S(1)}, f32[64,64]{1,0:T(8,128)S(1)}, u32[]{:S(2)}, u32[]{:S(2)}) collective-permute-start(f32[64,64]{1,0:T(8,128)S(1)} %add.26), channel_id=1, source_target_pairs={{0,96},{1,97},{2,98},{3,99},{4,100},{5,101},{6,102},{7,103},{8,104... | collective-permute-start | bytes 49160 | tf_op jit(solution)/shard_map/ppermute | solution.py:163
  124.9 3.8 %collective-permute-done.6 = f32[64,64]{1,0:T(8,128)S(1)} collective-permute-done((f32[64,64]{1,0:T(8,128)S(1)}, f32[64,64]{1,0:T(8,128)S(1)}, u32[]{:S(2)}, u32[]{:S(2)}) %collective-permute-start.6) | collective-permute-done | bytes 16416 | tf_op jit(solution)/shard_map/ppermute | solution.py:163
  128.7 0.6 add_multiply_fusion
  (5 shorter events, 0.0 us)
Async XLA Ops:
  5.8 64.3 %all-to-all-start = ((bf16[128,4,32,128]{3,2,1,0:T(8,128)(2,1)}), bf16[128,4,32,128]{3,2,1,0:T(8,128)(2,1)}, u32[]{:S(2)}, u32[]{:S(2)}) async-start(bf16[128,4,32,128]{3,2,1,0:T(8,128)(2,1)} %bitcast.11), calls=%async_computation | async-start | bytes 8388608 | tf_op jit(solution)/shard_map/all_to_all | solution.py:152
  99.4 1.4 %collective-permute-start = (f32[64,64]{1,0:T(8,128)}, f32[64,64]{1,0:T(8,128)S(1)}, u32[]{:S(2)}, u32[]{:S(2)}) collective-permute-start(f32[64,64]{1,0:T(8,128)} %get-tuple-element.5), channel_id=1, source_target_pairs={{0,1},{1,0},{2,3},{3,2},{4,5},{5,4},{6,7},{7,6},{8,9},{9,8},{10,11... | collective-permute-start | bytes 49160 | tf_op jit(solution)/shard_map/ppermute | solution.py:163
  101.6 3.9 %collective-permute-start.1 = (f32[64,64]{1,0:T(8,128)S(1)}, f32[64,64]{1,0:T(8,128)S(1)}, u32[]{:S(2)}, u32[]{:S(2)}) collective-permute-start(f32[64,64]{1,0:T(8,128)S(1)} %add.21), channel_id=1, source_target_pairs={{0,2},{1,3},{2,0},{3,1},{4,6},{5,7},{6,4},{7,5},{8,10},{9,11},{10,... | collective-permute-start | bytes 49160 | tf_op jit(solution)/shard_map/ppermute | solution.py:163
  105.5 5.1 %collective-permute-start.2 = (f32[64,64]{1,0:T(8,128)S(1)}, f32[64,64]{1,0:T(8,128)S(1)}, u32[]{:S(2)}, u32[]{:S(2)}) collective-permute-start(f32[64,64]{1,0:T(8,128)S(1)} %add.22), channel_id=1, source_target_pairs={{0,6},{1,7},{2,4},{3,5},{4,2},{5,3},{6,0},{7,1},{8,14},{9,15},{10,... | collective-permute-start | bytes 49160 | tf_op jit(solution)/shard_map/ppermute | solution.py:163
  110.6 3.9 %collective-permute-start.3 = (f32[64,64]{1,0:T(8,128)S(1)}, f32[64,64]{1,0:T(8,128)S(1)}, u32[]{:S(2)}, u32[]{:S(2)}) collective-permute-start(f32[64,64]{1,0:T(8,128)S(1)} %add.23), channel_id=1, source_target_pairs={{0,8},{1,9},{2,10},{3,11},{4,12},{5,13},{6,14},{7,15},{8,0},{9,1},... | collective-permute-start | bytes 49160 | tf_op jit(solution)/shard_map/ppermute | solution.py:163
  114.6 5.1 %collective-permute-start.4 = (f32[64,64]{1,0:T(8,128)S(1)}, f32[64,64]{1,0:T(8,128)S(1)}, u32[]{:S(2)}, u32[]{:S(2)}) collective-permute-start(f32[64,64]{1,0:T(8,128)S(1)} %add.24), channel_id=1, source_target_pairs={{0,24},{1,25},{2,26},{3,27},{4,28},{5,29},{6,30},{7,31},{8,16},{9,... | collective-permute-start | bytes 49160 | tf_op jit(solution)/shard_map/ppermute | solution.py:163
  119.7 3.9 %collective-permute-start.5 = (f32[64,64]{1,0:T(8,128)S(1)}, f32[64,64]{1,0:T(8,128)S(1)}, u32[]{:S(2)}, u32[]{:S(2)}) collective-permute-start(f32[64,64]{1,0:T(8,128)S(1)} %add.25), channel_id=1, source_target_pairs={{0,32},{1,33},{2,34},{3,35},{4,36},{5,37},{6,38},{7,39},{8,40},{9,... | collective-permute-start | bytes 49160 | tf_op jit(solution)/shard_map/ppermute | solution.py:163
  123.6 5.1 %collective-permute-start.6 = (f32[64,64]{1,0:T(8,128)S(1)}, f32[64,64]{1,0:T(8,128)S(1)}, u32[]{:S(2)}, u32[]{:S(2)}) collective-permute-start(f32[64,64]{1,0:T(8,128)S(1)} %add.26), channel_id=1, source_target_pairs={{0,96},{1,97},{2,98},{3,99},{4,100},{5,101},{6,102},{7,103},{8,104... | collective-permute-start | bytes 49160 | tf_op jit(solution)/shard_map/ppermute | solution.py:163

commit v7 on v5

--- a/solution.py
+++ b/solution.py
@@ -11,7 +11,7 @@
 MODES = 64
 SLOTS = 7
 ROW_TILE = 64
-SEND_STEPS = 4
+SEND_STEPS = 8
 
 
 def gather_outgoing(pod_basis, picks_by_ghost):

time: 129 us -> 130 us (level)
  no operation moved by 1% of the time
where the time goes in v7:
time: 130 us
  waiting for transfers between devices  66.2 us (51%)
  Pallas kernels  45.9 us (35%)
  starting transfers between devices  15.4 us (12%)
  other arithmetic  1.41 us (1%)
    all_to_all x1, waiting for transfers between devices, on_device(): lax.all_to_all(outgoing, ('dom', 'outer'), split_axis=0, concat_axis=0, t...  41.4 us
    pallas_call x1, Pallas kernels, block_products(): pl.pallas_call(body, grid_spec=grid_spec, out_shape=(jax.ShapeDtypeStruct...  28.5 us
    ppermute x7, waiting for transfers between devices, on_device(): total = total + lax.ppermute(total, ('dom', 'outer'), pairs)  24.8 us
    all_to_all x1, starting transfers between devices, on_device(): lax.all_to_all(outgoing, ('dom', 'outer'), split_axis=0, concat_axis=0, t...  11.7 us
    pallas_call x1, Pallas kernels, relayout_jacobian(): pl.pallas_call(body, grid=(rows // tile,), in_specs=[pl.BlockSpec((slots,...  11.2 us
    pallas_call x1, Pallas kernels, gather_outgoing(): pl.pallas_call(body, grid_spec=grid_spec, out_shape=jax.ShapeDtypeStruct(...  6.21 us
    ppermute x7, starting transfers between devices, on_device(): total = total + lax.ppermute(total, ('dom', 'outer'), pairs)  3.69 us
  transfers between devices with their start and end apart: 8, of which 8 were waited for; matrix products, arithmetic and copies ran while one was open for 0% of the time, Pallas kernels for 9%

profile of v7, /device:TPU:0, one launch (start us, length us, event | category | flops | bytes accessed | tf_op | source)
XLA Modules:
  0.0 129.6 jit_solution(6810418987637254042)
XLA Ops:
  0.6 6.2 %shard_map.60 = bf16[512,32,128]{2,1,0:T(8,128)(2,1)} custom-call(s32[512]{0:T(512)} %bitcast.14, bf16[128,4096]{1,0:T(8,128)(2,1)} %pod_ref.1), custom_call_target="tpu_custom_call" | custom-call | tf_op jit(solution)/shard_map/pallas_call | solution.py:49
  6.8 11.7 %all-to-all-start = ((bf16[128,4,32,128]{3,2,1,0:T(8,128)(2,1)}), bf16[128,4,32,128]{3,2,1,0:T(8,128)(2,1)}, u32[]{:S(2)}, u32[]{:S(2)}) async-start(bf16[128,4,32,128]{3,2,1,0:T(8,128)(2,1)} %bitcast.11), calls=%async_computation | async-start | bytes 8388608 | tf_op jit(solution)/shard_map/all_to_all | solution.py:151
  18.5 11.2 %shard_map.59.jac_ref = bf16[7,128,64,64]{3,2,1,0:T(8,128)(2,1)} custom-call(bf16[7,128,4096]{2,1,0:T(8,128)(2,1)} %bitcast.12), custom_call_target="tpu_custom_call" | custom-call | tf_op jit(solution)/shard_map/pallas_call | solution.py:65
  29.7 41.4 %all-to-all-done = bf16[128,4,32,128]{3,2,1,0:T(8,128)(2,1)} async-done(((bf16[128,4,32,128]{3,2,1,0:T(8,128)(2,1)}), bf16[128,4,32,128]{3,2,1,0:T(8,128)(2,1)}, u32[]{:S(2)}, u32[]{:S(2)}) %all-to-all-start) | async-done | bytes 4194336 | tf_op jit(solution)/shard_map/all_to_all | solution.py:151
  71.1 28.5 %shard_map.61 = (bf16[128,4096]{1,0:T(8,128)(2,1)}, f32[64,64]{1,0:T(8,128)}) custom-call(s32[896]{0:T(1024)} %bitcast.13, bf16[7,128,64,64]{3,2,1,0:T(8,128)(2,1)} %shard_map.59.jac_ref, bf16[512,32,128]{2,1,0:T(8,128)(2,1)} %bitcast.7.tab_ref), custom_call_target="tpu_custom_call" | custom-call | tf_op jit(solution)/shard_map/pallas_call | solution.py:131
  99.6 0.0 collective-permute-start
  99.6 1.4 %collective-permute-done = f32[64,64]{1,0:T(8,128)S(1)} collective-permute-done((f32[64,64]{1,0:T(8,128)}, f32[64,64]{1,0:T(8,128)S(1)}, u32[]{:S(2)}, u32[]{:S(2)}) %collective-permute-start) | collective-permute-done | bytes 16416 | tf_op jit(solution)/shard_map/ppermute | solution.py:162
  101.0 0.8 add.21
  101.8 0.4 collective-permute-start.1
  102.2 3.5 %collective-permute-done.1 = f32[64,64]{1,0:T(8,128)S(1)} collective-permute-done((f32[64,64]{1,0:T(8,128)S(1)}, f32[64,64]{1,0:T(8,128)S(1)}, u32[]{:S(2)}, u32[]{:S(2)}) %collective-permute-start.1) | collective-permute-done | bytes 16416 | tf_op jit(solution)/shard_map/ppermute | solution.py:162
  105.7 0.4 collective-permute-start.2
  106.1 4.7 %collective-permute-done.2 = f32[64,64]{1,0:T(8,128)S(1)} collective-permute-done((f32[64,64]{1,0:T(8,128)S(1)}, f32[64,64]{1,0:T(8,128)S(1)}, u32[]{:S(2)}, u32[]{:S(2)}) %collective-permute-start.2) | collective-permute-done | bytes 16416 | tf_op jit(solution)/shard_map/ppermute | solution.py:162
  110.9 0.6 collective-permute-start.3
  111.4 3.3 %collective-permute-done.3 = f32[64,64]{1,0:T(8,128)S(1)} collective-permute-done((f32[64,64]{1,0:T(8,128)S(1)}, f32[64,64]{1,0:T(8,128)S(1)}, u32[]{:S(2)}, u32[]{:S(2)}) %collective-permute-start.3) | collective-permute-done | bytes 16416 | tf_op jit(solution)/shard_map/ppermute | solution.py:162
  114.8 0.5 collective-permute-start.4
  115.3 4.6 %collective-permute-done.4 = f32[64,64]{1,0:T(8,128)S(1)} collective-permute-done((f32[64,64]{1,0:T(8,128)S(1)}, f32[64,64]{1,0:T(8,128)S(1)}, u32[]{:S(2)}, u32[]{:S(2)}) %collective-permute-start.4) | collective-permute-done | bytes 16416 | tf_op jit(solution)/shard_map/ppermute | solution.py:162
  119.9 0.5 collective-permute-start.5
  120.4 3.4 %collective-permute-done.5 = f32[64,64]{1,0:T(8,128)S(1)} collective-permute-done((f32[64,64]{1,0:T(8,128)S(1)}, f32[64,64]{1,0:T(8,128)S(1)}, u32[]{:S(2)}, u32[]{:S(2)}) %collective-permute-start.5) | collective-permute-done | bytes 16416 | tf_op jit(solution)/shard_map/ppermute | solution.py:162
  123.8 1.3 %collective-permute-start.6 = (f32[64,64]{1,0:T(8,128)S(1)}, f32[64,64]{1,0:T(8,128)S(1)}, u32[]{:S(2)}, u32[]{:S(2)}) collective-permute-start(f32[64,64]{1,0:T(8,128)S(1)} %add.26), channel_id=1, source_target_pairs={{0,96},{1,97},{2,98},{3,99},{4,100},{5,101},{6,102},{7,103},{8,104... | collective-permute-start | bytes 49160 | tf_op jit(solution)/shard_map/ppermute | solution.py:162
  125.1 3.8 %collective-permute-done.6 = f32[64,64]{1,0:T(8,128)S(1)} collective-permute-done((f32[64,64]{1,0:T(8,128)S(1)}, f32[64,64]{1,0:T(8,128)S(1)}, u32[]{:S(2)}, u32[]{:S(2)}) %collective-permute-start.6) | collective-permute-done | bytes 16416 | tf_op jit(solution)/shard_map/ppermute | solution.py:162
  129.0 0.6 add_multiply_fusion
  (5 shorter events, 0.0 us)
Async XLA Ops:
  6.8 64.3 %all-to-all-start = ((bf16[128,4,32,128]{3,2,1,0:T(8,128)(2,1)}), bf16[128,4,32,128]{3,2,1,0:T(8,128)(2,1)}, u32[]{:S(2)}, u32[]{:S(2)}) async-start(bf16[128,4,32,128]{3,2,1,0:T(8,128)(2,1)} %bitcast.11), calls=%async_computation | async-start | bytes 8388608 | tf_op jit(solution)/shard_map/all_to_all | solution.py:151
  99.6 1.4 %collective-permute-start = (f32[64,64]{1,0:T(8,128)}, f32[64,64]{1,0:T(8,128)S(1)}, u32[]{:S(2)}, u32[]{:S(2)}) collective-permute-start(f32[64,64]{1,0:T(8,128)} %get-tuple-element.5), channel_id=1, source_target_pairs={{0,1},{1,0},{2,3},{3,2},{4,5},{5,4},{6,7},{7,6},{8,9},{9,8},{10,11... | collective-permute-start | bytes 49160 | tf_op jit(solution)/shard_map/ppermute | solution.py:162
  101.8 3.9 %collective-permute-start.1 = (f32[64,64]{1,0:T(8,128)S(1)}, f32[64,64]{1,0:T(8,128)S(1)}, u32[]{:S(2)}, u32[]{:S(2)}) collective-permute-start(f32[64,64]{1,0:T(8,128)S(1)} %add.21), channel_id=1, source_target_pairs={{0,2},{1,3},{2,0},{3,1},{4,6},{5,7},{6,4},{7,5},{8,10},{9,11},{10,... | collective-permute-start | bytes 49160 | tf_op jit(solution)/shard_map/ppermute | solution.py:162
  105.7 5.1 %collective-permute-start.2 = (f32[64,64]{1,0:T(8,128)S(1)}, f32[64,64]{1,0:T(8,128)S(1)}, u32[]{:S(2)}, u32[]{:S(2)}) collective-permute-start(f32[64,64]{1,0:T(8,128)S(1)} %add.22), channel_id=1, source_target_pairs={{0,6},{1,7},{2,4},{3,5},{4,2},{5,3},{6,0},{7,1},{8,14},{9,15},{10,... | collective-permute-start | bytes 49160 | tf_op jit(solution)/shard_map/ppermute | solution.py:162
  110.9 3.9 %collective-permute-start.3 = (f32[64,64]{1,0:T(8,128)S(1)}, f32[64,64]{1,0:T(8,128)S(1)}, u32[]{:S(2)}, u32[]{:S(2)}) collective-permute-start(f32[64,64]{1,0:T(8,128)S(1)} %add.23), channel_id=1, source_target_pairs={{0,8},{1,9},{2,10},{3,11},{4,12},{5,13},{6,14},{7,15},{8,0},{9,1},... | collective-permute-start | bytes 49160 | tf_op jit(solution)/shard_map/ppermute | solution.py:162
  114.8 5.1 %collective-permute-start.4 = (f32[64,64]{1,0:T(8,128)S(1)}, f32[64,64]{1,0:T(8,128)S(1)}, u32[]{:S(2)}, u32[]{:S(2)}) collective-permute-start(f32[64,64]{1,0:T(8,128)S(1)} %add.24), channel_id=1, source_target_pairs={{0,24},{1,25},{2,26},{3,27},{4,28},{5,29},{6,30},{7,31},{8,16},{9,... | collective-permute-start | bytes 49160 | tf_op jit(solution)/shard_map/ppermute | solution.py:162
  119.9 3.9 %collective-permute-start.5 = (f32[64,64]{1,0:T(8,128)S(1)}, f32[64,64]{1,0:T(8,128)S(1)}, u32[]{:S(2)}, u32[]{:S(2)}) collective-permute-start(f32[64,64]{1,0:T(8,128)S(1)} %add.25), channel_id=1, source_target_pairs={{0,32},{1,33},{2,34},{3,35},{4,36},{5,37},{6,38},{7,39},{8,40},{9,... | collective-permute-start | bytes 49160 | tf_op jit(solution)/shard_map/ppermute | solution.py:162
  123.8 5.1 %collective-permute-start.6 = (f32[64,64]{1,0:T(8,128)S(1)}, f32[64,64]{1,0:T(8,128)S(1)}, u32[]{:S(2)}, u32[]{:S(2)}) collective-permute-start(f32[64,64]{1,0:T(8,128)S(1)} %add.26), channel_id=1, source_target_pairs={{0,96},{1,97},{2,98},{3,99},{4,100},{5,101},{6,102},{7,103},{8,104... | collective-permute-start | bytes 49160 | tf_op jit(solution)/shard_map/ppermute | solution.py:162

commit v8 on v5

--- a/solution.py
+++ b/solution.py
@@ -71,7 +71,7 @@
     )(jac_by_slot)
 
 
-def block_products(jac_by_slot, table, column_slot):
+def block_products(jac_by_slot, table, column_slot, scale):
     slots, rows = jac_by_slot.shape[:2]
     block_area = BLOCK * MODES
     entries = table.shape[0]
@@ -108,7 +108,7 @@
             )
         rounded = acc.astype(jnp.bfloat16)
         out_ref[...] = rounded.reshape(tile, block_area)
-        part_ref[...] += lax.dot_general(
+        part_ref[...] += scale * lax.dot_general(
             diag.reshape(tile * BLOCK, MODES),
             rounded.reshape(tile * BLOCK, MODES),
             (((0,), (0,)), ((), ())),
@@ -151,7 +151,8 @@
     received = lax.all_to_all(outgoing, ("dom", "outer"), split_axis=0, concat_axis=0, tiled=True)
     table = received.reshape((device_count * ghost_count,) + received.shape[2:])
     jac_by_slot = relayout_jacobian(jnp.transpose(jacobian, (1, 0, 2)))
-    galerkin_rows, partial_value = block_products(jac_by_slot, table, column_slot)
+    scale = 1.0 / math.sqrt(rows_local * device_count * BLOCK)
+    galerkin_rows, partial_value = block_products(jac_by_slot, table, column_slot, scale)
     total = partial_value
     for stride, span in ((1, 2), (2, 4), (8, 4), (32, 4)):
         for flip in ((lambda d: 1 - d),) if span == 2 else ((lambda d: d ^ 1), (lambda d: 3 - d)):
@@ -160,7 +161,7 @@
                 digit = (i // stride) % span
                 pairs.append((i, i + (flip(digit) - digit) * stride))
             total = total + lax.ppermute(total, ("dom", "outer"), pairs)
-    reduced = total / math.sqrt(rows_local * device_count * BLOCK)
+    reduced = total
     return (galerkin_rows, reduced)
 
 

time: 129 us -> 129 us (level)
  no operation moved by 1% of the time
where the time goes in v8:
time: 129 us
  waiting for transfers between devices  66.2 us (51%)
  Pallas kernels  44.8 us (35%)
  starting transfers between devices  15.4 us (12%)
  other arithmetic  1.41 us (1%)
    all_to_all x1, waiting for transfers between devices, on_device(): lax.all_to_all(outgoing, ('dom', 'outer'), split_axis=0, concat_axis=0, t...  41.4 us
    pallas_call x1, Pallas kernels, block_products(): pl.pallas_call(body, grid_spec=grid_spec, out_shape=(jax.ShapeDtypeStruct...  28.5 us
    ppermute x7, waiting for transfers between devices, on_device(): total = total + lax.ppermute(total, ('dom', 'outer'), pairs)  24.8 us
    all_to_all x1, starting transfers between devices, on_device(): lax.all_to_all(outgoing, ('dom', 'outer'), split_axis=0, concat_axis=0, t...  11.7 us
    pallas_call x1, Pallas kernels, relayout_jacobian(): pl.pallas_call(body, grid=(rows // tile,), in_specs=[pl.BlockSpec((slots,...  11.2 us
    pallas_call x1, Pallas kernels, gather_outgoing(): pl.pallas_call(body, grid_spec=grid_spec, out_shape=jax.ShapeDtypeStruct(...  5.14 us
    ppermute x7, starting transfers between devices, on_device(): total = total + lax.ppermute(total, ('dom', 'outer'), pairs)  3.69 us
  transfers between devices with their start and end apart: 8, of which 8 were waited for; matrix products, arithmetic and copies ran while one was open for 0% of the time, Pallas kernels for 9%

profile of v8, /device:TPU:0, one launch (start us, length us, event | category | flops | bytes accessed | tf_op | source)
XLA Modules:
  0.0 128.5 jit_solution(504139257220199712)
XLA Ops:
  0.6 5.1 %shard_map.60 = bf16[512,32,128]{2,1,0:T(8,128)(2,1)} custom-call(s32[512]{0:T(512)} %bitcast.14, bf16[128,4096]{1,0:T(8,128)(2,1)} %pod_ref.1), custom_call_target="tpu_custom_call" | custom-call | tf_op jit(solution)/shard_map/pallas_call | solution.py:49
  5.8 11.7 %all-to-all-start = ((bf16[128,4,32,128]{3,2,1,0:T(8,128)(2,1)}), bf16[128,4,32,128]{3,2,1,0:T(8,128)(2,1)}, u32[]{:S(2)}, u32[]{:S(2)}) async-start(bf16[128,4,32,128]{3,2,1,0:T(8,128)(2,1)} %bitcast.11), calls=%async_computation | async-start | bytes 8388608 | tf_op jit(solution)/shard_map/all_to_all | solution.py:151
  17.5 11.2 %shard_map.59.jac_ref = bf16[7,128,64,64]{3,2,1,0:T(8,128)(2,1)} custom-call(bf16[7,128,4096]{2,1,0:T(8,128)(2,1)} %bitcast.12), custom_call_target="tpu_custom_call" | custom-call | tf_op jit(solution)/shard_map/pallas_call | solution.py:65
  28.7 41.4 %all-to-all-done = bf16[128,4,32,128]{3,2,1,0:T(8,128)(2,1)} async-done(((bf16[128,4,32,128]{3,2,1,0:T(8,128)(2,1)}), bf16[128,4,32,128]{3,2,1,0:T(8,128)(2,1)}, u32[]{:S(2)}, u32[]{:S(2)}) %all-to-all-start) | async-done | bytes 4194336 | tf_op jit(solution)/shard_map/all_to_all | solution.py:151
  70.1 28.5 %shard_map.61 = (bf16[128,4096]{1,0:T(8,128)(2,1)}, f32[64,64]{1,0:T(8,128)}) custom-call(s32[896]{0:T(1024)} %bitcast.13, bf16[7,128,64,64]{3,2,1,0:T(8,128)(2,1)} %shard_map.59.jac_ref, bf16[512,32,128]{2,1,0:T(8,128)(2,1)} %bitcast.7.tab_ref), custom_call_target="tpu_custom_call" | custom-call | tf_op jit(solution)/shard_map/pallas_call | solution.py:131
  98.6 0.0 collective-permute-start
  98.6 1.4 %collective-permute-done = f32[64,64]{1,0:T(8,128)S(1)} collective-permute-done((f32[64,64]{1,0:T(8,128)}, f32[64,64]{1,0:T(8,128)S(1)}, u32[]{:S(2)}, u32[]{:S(2)}) %collective-permute-start) | collective-permute-done | bytes 16416 | tf_op jit(solution)/shard_map/ppermute | solution.py:163
  100.0 0.8 add.21
  100.8 0.4 collective-permute-start.1
  101.2 3.5 %collective-permute-done.1 = f32[64,64]{1,0:T(8,128)S(1)} collective-permute-done((f32[64,64]{1,0:T(8,128)S(1)}, f32[64,64]{1,0:T(8,128)S(1)}, u32[]{:S(2)}, u32[]{:S(2)}) %collective-permute-start.1) | collective-permute-done | bytes 16416 | tf_op jit(solution)/shard_map/ppermute | solution.py:163
  104.7 0.4 collective-permute-start.2
  105.1 4.7 %collective-permute-done.2 = f32[64,64]{1,0:T(8,128)S(1)} collective-permute-done((f32[64,64]{1,0:T(8,128)S(1)}, f32[64,64]{1,0:T(8,128)S(1)}, u32[]{:S(2)}, u32[]{:S(2)}) %collective-permute-start.2) | collective-permute-done | bytes 16416 | tf_op jit(solution)/shard_map/ppermute | solution.py:163
  109.8 0.6 collective-permute-start.3
  110.4 3.3 %collective-permute-done.3 = f32[64,64]{1,0:T(8,128)S(1)} collective-permute-done((f32[64,64]{1,0:T(8,128)S(1)}, f32[64,64]{1,0:T(8,128)S(1)}, u32[]{:S(2)}, u32[]{:S(2)}) %collective-permute-start.3) | collective-permute-done | bytes 16416 | tf_op jit(solution)/shard_map/ppermute | solution.py:163
  113.7 0.5 collective-permute-start.4
  114.2 4.6 %collective-permute-done.4 = f32[64,64]{1,0:T(8,128)S(1)} collective-permute-done((f32[64,64]{1,0:T(8,128)S(1)}, f32[64,64]{1,0:T(8,128)S(1)}, u32[]{:S(2)}, u32[]{:S(2)}) %collective-permute-start.4) | collective-permute-done | bytes 16416 | tf_op jit(solution)/shard_map/ppermute | solution.py:163
  118.9 0.5 collective-permute-start.5
  119.4 3.4 %collective-permute-done.5 = f32[64,64]{1,0:T(8,128)S(1)} collective-permute-done((f32[64,64]{1,0:T(8,128)S(1)}, f32[64,64]{1,0:T(8,128)S(1)}, u32[]{:S(2)}, u32[]{:S(2)}) %collective-permute-start.5) | collective-permute-done | bytes 16416 | tf_op jit(solution)/shard_map/ppermute | solution.py:163
  122.8 1.3 %collective-permute-start.6 = (f32[64,64]{1,0:T(8,128)S(1)}, f32[64,64]{1,0:T(8,128)S(1)}, u32[]{:S(2)}, u32[]{:S(2)}) collective-permute-start(f32[64,64]{1,0:T(8,128)S(1)} %add.26), channel_id=1, source_target_pairs={{0,96},{1,97},{2,98},{3,99},{4,100},{5,101},{6,102},{7,103},{8,104... | collective-permute-start | bytes 49160 | tf_op jit(solution)/shard_map/ppermute | solution.py:163
  124.1 3.8 %collective-permute-done.6 = f32[64,64]{1,0:T(8,128)S(1)} collective-permute-done((f32[64,64]{1,0:T(8,128)S(1)}, f32[64,64]{1,0:T(8,128)S(1)}, u32[]{:S(2)}, u32[]{:S(2)}) %collective-permute-start.6) | collective-permute-done | bytes 16416 | tf_op jit(solution)/shard_map/ppermute | solution.py:163
  127.9 0.6 add.27
  (5 shorter events, 0.0 us)
Async XLA Ops:
  5.8 64.3 %all-to-all-start = ((bf16[128,4,32,128]{3,2,1,0:T(8,128)(2,1)}), bf16[128,4,32,128]{3,2,1,0:T(8,128)(2,1)}, u32[]{:S(2)}, u32[]{:S(2)}) async-start(bf16[128,4,32,128]{3,2,1,0:T(8,128)(2,1)} %bitcast.11), calls=%async_computation | async-start | bytes 8388608 | tf_op jit(solution)/shard_map/all_to_all | solution.py:151
  98.6 1.4 %collective-permute-start = (f32[64,64]{1,0:T(8,128)}, f32[64,64]{1,0:T(8,128)S(1)}, u32[]{:S(2)}, u32[]{:S(2)}) collective-permute-start(f32[64,64]{1,0:T(8,128)} %get-tuple-element.5), channel_id=1, source_target_pairs={{0,1},{1,0},{2,3},{3,2},{4,5},{5,4},{6,7},{7,6},{8,9},{9,8},{10,11... | collective-permute-start | bytes 49160 | tf_op jit(solution)/shard_map/ppermute | solution.py:163
  100.8 3.9 %collective-permute-start.1 = (f32[64,64]{1,0:T(8,128)S(1)}, f32[64,64]{1,0:T(8,128)S(1)}, u32[]{:S(2)}, u32[]{:S(2)}) collective-permute-start(f32[64,64]{1,0:T(8,128)S(1)} %add.21), channel_id=1, source_target_pairs={{0,2},{1,3},{2,0},{3,1},{4,6},{5,7},{6,4},{7,5},{8,10},{9,11},{10,... | collective-permute-start | bytes 49160 | tf_op jit(solution)/shard_map/ppermute | solution.py:163
  104.7 5.1 %collective-permute-start.2 = (f32[64,64]{1,0:T(8,128)S(1)}, f32[64,64]{1,0:T(8,128)S(1)}, u32[]{:S(2)}, u32[]{:S(2)}) collective-permute-start(f32[64,64]{1,0:T(8,128)S(1)} %add.22), channel_id=1, source_target_pairs={{0,6},{1,7},{2,4},{3,5},{4,2},{5,3},{6,0},{7,1},{8,14},{9,15},{10,... | collective-permute-start | bytes 49160 | tf_op jit(solution)/shard_map/ppermute | solution.py:163
  109.8 3.9 %collective-permute-start.3 = (f32[64,64]{1,0:T(8,128)S(1)}, f32[64,64]{1,0:T(8,128)S(1)}, u32[]{:S(2)}, u32[]{:S(2)}) collective-permute-start(f32[64,64]{1,0:T(8,128)S(1)} %add.23), channel_id=1, source_target_pairs={{0,8},{1,9},{2,10},{3,11},{4,12},{5,13},{6,14},{7,15},{8,0},{9,1},... | collective-permute-start | bytes 49160 | tf_op jit(solution)/shard_map/ppermute | solution.py:163
  113.7 5.1 %collective-permute-start.4 = (f32[64,64]{1,0:T(8,128)S(1)}, f32[64,64]{1,0:T(8,128)S(1)}, u32[]{:S(2)}, u32[]{:S(2)}) collective-permute-start(f32[64,64]{1,0:T(8,128)S(1)} %add.24), channel_id=1, source_target_pairs={{0,24},{1,25},{2,26},{3,27},{4,28},{5,29},{6,30},{7,31},{8,16},{9,... | collective-permute-start | bytes 49160 | tf_op jit(solution)/shard_map/ppermute | solution.py:163
  118.9 3.9 %collective-permute-start.5 = (f32[64,64]{1,0:T(8,128)S(1)}, f32[64,64]{1,0:T(8,128)S(1)}, u32[]{:S(2)}, u32[]{:S(2)}) collective-permute-start(f32[64,64]{1,0:T(8,128)S(1)} %add.25), channel_id=1, source_target_pairs={{0,32},{1,33},{2,34},{3,35},{4,36},{5,37},{6,38},{7,39},{8,40},{9,... | collective-permute-start | bytes 49160 | tf_op jit(solution)/shard_map/ppermute | solution.py:163
  122.8 5.1 %collective-permute-start.6 = (f32[64,64]{1,0:T(8,128)S(1)}, f32[64,64]{1,0:T(8,128)S(1)}, u32[]{:S(2)}, u32[]{:S(2)}) collective-permute-start(f32[64,64]{1,0:T(8,128)S(1)} %add.26), channel_id=1, source_target_pairs={{0,96},{1,97},{2,98},{3,99},{4,100},{5,101},{6,102},{7,103},{8,104... | collective-permute-start | bytes 49160 | tf_op jit(solution)/shard_map/ppermute | solution.py:163

commit v9 on v8

--- a/solution.py
+++ b/solution.py
@@ -37,7 +37,7 @@
                 out_ref[dl * ghosts + g] = slab_ref[pick_ref[g * dests + d]]
             return carry
 
-        lax.fori_loop(0, dests_per_step, one, 0, unroll=4)
+        lax.fori_loop(0, dests_per_step, one, 0, unroll=8)
 
     grid_spec = pltpu.PrefetchScalarGridSpec(
         num_scalar_prefetch=1,

time: 129 us -> 129 us (level)
  no operation moved by 1% of the time
where the time goes in v9:
time: 129 us; the launch traced here: 128 us
  waiting for transfers between devices  66.2 us (51%)
  Pallas kernels  44.8 us (35%)
  starting transfers between devices  15.4 us (12%)
  other arithmetic  1.41 us (1%)
    all_to_all x1, waiting for transfers between devices, on_device(): lax.all_to_all(outgoing, ('dom', 'outer'), split_axis=0, concat_axis=0, t...  41.4 us
    pallas_call x1, Pallas kernels, block_products(): pl.pallas_call(body, grid_spec=grid_spec, out_shape=(jax.ShapeDtypeStruct...  28.5 us
    ppermute x7, waiting for transfers between devices, on_device(): total = total + lax.ppermute(total, ('dom', 'outer'), pairs)  24.9 us
    all_to_all x1, starting transfers between devices, on_device(): lax.all_to_all(outgoing, ('dom', 'outer'), split_axis=0, concat_axis=0, t...  11.7 us
    pallas_call x1, Pallas kernels, relayout_jacobian(): pl.pallas_call(body, grid=(rows // tile,), in_specs=[pl.BlockSpec((slots,...  11.2 us
    pallas_call x1, Pallas kernels, gather_outgoing(): pl.pallas_call(body, grid_spec=grid_spec, out_shape=jax.ShapeDtypeStruct(...  5.1 us
    ppermute x7, starting transfers between devices, on_device(): total = total + lax.ppermute(total, ('dom', 'outer'), pairs)  3.68 us
  transfers between devices with their start and end apart: 8, of which 8 were waited for; matrix products, arithmetic and copies ran while one was open for 0% of the time, Pallas kernels for 9%

profile of v9, /device:TPU:0, one launch (start us, length us, event | category | flops | bytes accessed | tf_op | source)
XLA Modules:
  0.0 128.5 jit_solution(4447368047097438438)
XLA Ops:
  0.6 5.1 %shard_map.60 = bf16[512,32,128]{2,1,0:T(8,128)(2,1)} custom-call(s32[512]{0:T(512)} %bitcast.14, bf16[128,4096]{1,0:T(8,128)(2,1)} %pod_ref.1), custom_call_target="tpu_custom_call" | custom-call | tf_op jit(solution)/shard_map/pallas_call | solution.py:49
  5.7 11.7 %all-to-all-start = ((bf16[128,4,32,128]{3,2,1,0:T(8,128)(2,1)}), bf16[128,4,32,128]{3,2,1,0:T(8,128)(2,1)}, u32[]{:S(2)}, u32[]{:S(2)}) async-start(bf16[128,4,32,128]{3,2,1,0:T(8,128)(2,1)} %bitcast.11), calls=%async_computation | async-start | bytes 8388608 | tf_op jit(solution)/shard_map/all_to_all | solution.py:151
  17.4 11.2 %shard_map.59.jac_ref = bf16[7,128,64,64]{3,2,1,0:T(8,128)(2,1)} custom-call(bf16[7,128,4096]{2,1,0:T(8,128)(2,1)} %bitcast.12), custom_call_target="tpu_custom_call" | custom-call | tf_op jit(solution)/shard_map/pallas_call | solution.py:65
  28.6 41.4 %all-to-all-done = bf16[128,4,32,128]{3,2,1,0:T(8,128)(2,1)} async-done(((bf16[128,4,32,128]{3,2,1,0:T(8,128)(2,1)}), bf16[128,4,32,128]{3,2,1,0:T(8,128)(2,1)}, u32[]{:S(2)}, u32[]{:S(2)}) %all-to-all-start) | async-done | bytes 4194336 | tf_op jit(solution)/shard_map/all_to_all | solution.py:151
  70.0 28.5 %shard_map.61 = (bf16[128,4096]{1,0:T(8,128)(2,1)}, f32[64,64]{1,0:T(8,128)}) custom-call(s32[896]{0:T(1024)} %bitcast.13, bf16[7,128,64,64]{3,2,1,0:T(8,128)(2,1)} %shard_map.59.jac_ref, bf16[512,32,128]{2,1,0:T(8,128)(2,1)} %bitcast.7.tab_ref), custom_call_target="tpu_custom_call" | custom-call | tf_op jit(solution)/shard_map/pallas_call | solution.py:131
  98.5 0.0 collective-permute-start
  98.5 1.4 %collective-permute-done = f32[64,64]{1,0:T(8,128)S(1)} collective-permute-done((f32[64,64]{1,0:T(8,128)}, f32[64,64]{1,0:T(8,128)S(1)}, u32[]{:S(2)}, u32[]{:S(2)}) %collective-permute-start) | collective-permute-done | bytes 16416 | tf_op jit(solution)/shard_map/ppermute | solution.py:163
  99.9 0.8 add.21
  100.7 0.4 collective-permute-start.1
  101.1 3.5 %collective-permute-done.1 = f32[64,64]{1,0:T(8,128)S(1)} collective-permute-done((f32[64,64]{1,0:T(8,128)S(1)}, f32[64,64]{1,0:T(8,128)S(1)}, u32[]{:S(2)}, u32[]{:S(2)}) %collective-permute-start.1) | collective-permute-done | bytes 16416 | tf_op jit(solution)/shard_map/ppermute | solution.py:163
  104.6 0.4 collective-permute-start.2
  105.0 4.7 %collective-permute-done.2 = f32[64,64]{1,0:T(8,128)S(1)} collective-permute-done((f32[64,64]{1,0:T(8,128)S(1)}, f32[64,64]{1,0:T(8,128)S(1)}, u32[]{:S(2)}, u32[]{:S(2)}) %collective-permute-start.2) | collective-permute-done | bytes 16416 | tf_op jit(solution)/shard_map/ppermute | solution.py:163
  109.8 0.6 collective-permute-start.3
  110.3 3.4 %collective-permute-done.3 = f32[64,64]{1,0:T(8,128)S(1)} collective-permute-done((f32[64,64]{1,0:T(8,128)S(1)}, f32[64,64]{1,0:T(8,128)S(1)}, u32[]{:S(2)}, u32[]{:S(2)}) %collective-permute-start.3) | collective-permute-done | bytes 16416 | tf_op jit(solution)/shard_map/ppermute | solution.py:163
  113.7 0.5 collective-permute-start.4
  114.2 4.6 %collective-permute-done.4 = f32[64,64]{1,0:T(8,128)S(1)} collective-permute-done((f32[64,64]{1,0:T(8,128)S(1)}, f32[64,64]{1,0:T(8,128)S(1)}, u32[]{:S(2)}, u32[]{:S(2)}) %collective-permute-start.4) | collective-permute-done | bytes 16416 | tf_op jit(solution)/shard_map/ppermute | solution.py:163
  118.8 0.5 collective-permute-start.5
  119.3 3.4 %collective-permute-done.5 = f32[64,64]{1,0:T(8,128)S(1)} collective-permute-done((f32[64,64]{1,0:T(8,128)S(1)}, f32[64,64]{1,0:T(8,128)S(1)}, u32[]{:S(2)}, u32[]{:S(2)}) %collective-permute-start.5) | collective-permute-done | bytes 16416 | tf_op jit(solution)/shard_map/ppermute | solution.py:163
  122.7 1.3 %collective-permute-start.6 = (f32[64,64]{1,0:T(8,128)S(1)}, f32[64,64]{1,0:T(8,128)S(1)}, u32[]{:S(2)}, u32[]{:S(2)}) collective-permute-start(f32[64,64]{1,0:T(8,128)S(1)} %add.26), channel_id=1, source_target_pairs={{0,96},{1,97},{2,98},{3,99},{4,100},{5,101},{6,102},{7,103},{8,104... | collective-permute-start | bytes 49160 | tf_op jit(solution)/shard_map/ppermute | solution.py:163
  124.0 3.8 %collective-permute-done.6 = f32[64,64]{1,0:T(8,128)S(1)} collective-permute-done((f32[64,64]{1,0:T(8,128)S(1)}, f32[64,64]{1,0:T(8,128)S(1)}, u32[]{:S(2)}, u32[]{:S(2)}) %collective-permute-start.6) | collective-permute-done | bytes 16416 | tf_op jit(solution)/shard_map/ppermute | solution.py:163
  127.9 0.6 add.27
  (5 shorter events, 0.0 us)
Async XLA Ops:
  5.7 64.3 %all-to-all-start = ((bf16[128,4,32,128]{3,2,1,0:T(8,128)(2,1)}), bf16[128,4,32,128]{3,2,1,0:T(8,128)(2,1)}, u32[]{:S(2)}, u32[]{:S(2)}) async-start(bf16[128,4,32,128]{3,2,1,0:T(8,128)(2,1)} %bitcast.11), calls=%async_computation | async-start | bytes 8388608 | tf_op jit(solution)/shard_map/all_to_all | solution.py:151
  98.5 1.4 %collective-permute-start = (f32[64,64]{1,0:T(8,128)}, f32[64,64]{1,0:T(8,128)S(1)}, u32[]{:S(2)}, u32[]{:S(2)}) collective-permute-start(f32[64,64]{1,0:T(8,128)} %get-tuple-element.5), channel_id=1, source_target_pairs={{0,1},{1,0},{2,3},{3,2},{4,5},{5,4},{6,7},{7,6},{8,9},{9,8},{10,11... | collective-permute-start | bytes 49160 | tf_op jit(solution)/shard_map/ppermute | solution.py:163
  100.7 3.9 %collective-permute-start.1 = (f32[64,64]{1,0:T(8,128)S(1)}, f32[64,64]{1,0:T(8,128)S(1)}, u32[]{:S(2)}, u32[]{:S(2)}) collective-permute-start(f32[64,64]{1,0:T(8,128)S(1)} %add.21), channel_id=1, source_target_pairs={{0,2},{1,3},{2,0},{3,1},{4,6},{5,7},{6,4},{7,5},{8,10},{9,11},{10,... | collective-permute-start | bytes 49160 | tf_op jit(solution)/shard_map/ppermute | solution.py:163
  104.6 5.1 %collective-permute-start.2 = (f32[64,64]{1,0:T(8,128)S(1)}, f32[64,64]{1,0:T(8,128)S(1)}, u32[]{:S(2)}, u32[]{:S(2)}) collective-permute-start(f32[64,64]{1,0:T(8,128)S(1)} %add.22), channel_id=1, source_target_pairs={{0,6},{1,7},{2,4},{3,5},{4,2},{5,3},{6,0},{7,1},{8,14},{9,15},{10,... | collective-permute-start | bytes 49160 | tf_op jit(solution)/shard_map/ppermute | solution.py:163
  109.8 3.9 %collective-permute-start.3 = (f32[64,64]{1,0:T(8,128)S(1)}, f32[64,64]{1,0:T(8,128)S(1)}, u32[]{:S(2)}, u32[]{:S(2)}) collective-permute-start(f32[64,64]{1,0:T(8,128)S(1)} %add.23), channel_id=1, source_target_pairs={{0,8},{1,9},{2,10},{3,11},{4,12},{5,13},{6,14},{7,15},{8,0},{9,1},... | collective-permute-start | bytes 49160 | tf_op jit(solution)/shard_map/ppermute | solution.py:163
  113.7 5.1 %collective-permute-start.4 = (f32[64,64]{1,0:T(8,128)S(1)}, f32[64,64]{1,0:T(8,128)S(1)}, u32[]{:S(2)}, u32[]{:S(2)}) collective-permute-start(f32[64,64]{1,0:T(8,128)S(1)} %add.24), channel_id=1, source_target_pairs={{0,24},{1,25},{2,26},{3,27},{4,28},{5,29},{6,30},{7,31},{8,16},{9,... | collective-permute-start | bytes 49160 | tf_op jit(solution)/shard_map/ppermute | solution.py:163
  118.8 3.9 %collective-permute-start.5 = (f32[64,64]{1,0:T(8,128)S(1)}, f32[64,64]{1,0:T(8,128)S(1)}, u32[]{:S(2)}, u32[]{:S(2)}) collective-permute-start(f32[64,64]{1,0:T(8,128)S(1)} %add.25), channel_id=1, source_target_pairs={{0,32},{1,33},{2,34},{3,35},{4,36},{5,37},{6,38},{7,39},{8,40},{9,... | collective-permute-start | bytes 49160 | tf_op jit(solution)/shard_map/ppermute | solution.py:163
  122.7 5.1 %collective-permute-start.6 = (f32[64,64]{1,0:T(8,128)S(1)}, f32[64,64]{1,0:T(8,128)S(1)}, u32[]{:S(2)}, u32[]{:S(2)}) collective-permute-start(f32[64,64]{1,0:T(8,128)S(1)} %add.26), channel_id=1, source_target_pairs={{0,96},{1,97},{2,98},{3,99},{4,100},{5,101},{6,102},{7,103},{8,104... | collective-permute-start | bytes 49160 | tf_op jit(solution)/shard_map/ppermute | solution.py:163
